TPU v7x, 128 devices: a whole 4x4x4 slice. The times are simulated.
128 devices in a mesh: expert: 16 (over y, x), etp: 8 (over z, core).
Axes of the slice: x: 4, y: 4, z: 4, core: 2. Of those that a mesh axis runs over, the one named last changes fastest.
Arguments:
- tokens: bfloat16 [2048, 2048], P('expert'), may hold values from -6 to 6
- out_grad: bfloat16 [2048, 2048], P('expert'), may hold values from -6 to 6
- routes: int32 [2048, 2], P('expert'), may hold values from 0 to 15, as said below
- combine_weights: float32 [2048, 2], P('expert'), may hold values from 0.2 to 1
- w_gate: bfloat16 [16, 2048, 7168], P('expert', None, 'etp'), may hold values from -0.125 to 0.125
- w_up: bfloat16 [16, 2048, 7168], P('expert', None, 'etp'), may hold values from -0.125 to 0.125
- w_down: bfloat16 [16, 7168, 2048], P('expert', 'etp'), may hold values from -0.0625 to 0.0625
Outputs:
- mixed: bfloat16 [2048, 2048], P('expert')
- tokens_grad: bfloat16 [2048, 2048], P('expert')
- combine_grad: float32 [2048, 2], P('expert')
- gate_weight_grad: bfloat16 [16, 2048, 7168], P('expert', None, 'etp')
- up_weight_grad: bfloat16 [16, 2048, 7168], P('expert', None, 'etp')
- down_weight_grad: bfloat16 [16, 7168, 2048], P('expert', 'etp')
Inputs may be any that keep to these rules, and one draw needn't show every extreme that they name: `routes`: each token names two different experts. No expert is named by more than 32 tokens of one group of 128 consecutive tokens, and one expert, the same in every group, is named by exactly 32 tokens of each group.
All inputs are finite; a program needn't handle non-finite values.
Results may differ from a plain program's by a relative error of at most 0.02.
Values may be sent and summed in bfloat16 or wider, within the bound.
No kernel may reach another device: no remote copies, remote signals or barrier semaphores. Data moves between devices by JAX's collectives and lax.ppermute only.
A program may use at most 128 MiB of HBM per device.

v0:
```python
import jax
import jax.numpy as jnp
from jax import lax
from jax.sharding import PartitionSpec as P

TOP = 2


def contract_last(left, right):
    return lax.dot_general(
        left, right, (((1,), (1,)), ((), ())), preferred_element_type=jnp.float32
    )


def contract_first(left, right):
    return lax.dot_general(
        left, right, (((0,), (0,)), ((), ())), preferred_element_type=jnp.float32
    )


def select_rows(selector, table):
    return jnp.dot(selector.astype(table.dtype), table, preferred_element_type=jnp.float32)


def expert_rows(rows_in, rows_grad, gate_w, up_w, down_w):
    gate_pre = jnp.dot(rows_in, gate_w, preferred_element_type=jnp.float32)
    up_pre = jnp.dot(rows_in, up_w, preferred_element_type=jnp.float32)
    gate_sig = jax.nn.sigmoid(gate_pre)
    swish = gate_pre * gate_sig
    hidden = (swish * up_pre).astype(jnp.bfloat16)
    out_part = jnp.dot(hidden, down_w, preferred_element_type=jnp.float32)
    hidden_grad = contract_last(rows_grad, down_w)
    gate_grad = (hidden_grad * up_pre * gate_sig * (1.0 + gate_pre * (1.0 - gate_sig))).astype(
        jnp.bfloat16
    )
    up_grad = (hidden_grad * swish).astype(jnp.bfloat16)
    input_part = contract_last(gate_grad, gate_w) + contract_last(up_grad, up_w)
    return out_part, input_part, hidden, gate_grad, up_grad


def etp_perms(split_count):
    ring = split_count // 2
    swap = [(i, i ^ 1) for i in range(split_count)]
    onward = [(i, ((i // 2 + 1 - 2 * (i % 2)) % ring) * 2 + i % 2) for i in range(split_count)]
    backward = [(target, source) for source, target in onward]
    return swap, onward, backward


def etp_gather(unit, split_count, cover=None):
    swap, onward, _ = etp_perms(split_count)
    chip = jnp.stack([unit, lax.ppermute(unit, "etp", swap)], axis=1)
    first = lax.ppermute(chip, "etp", onward)
    if cover is not None:
        first, cover = lax.optimization_barrier((first, cover))
    second = lax.ppermute(first[:, 0], "etp", onward)
    held = jnp.concatenate([first, second[:, None]], axis=1)
    other = lax.ppermute(held, "etp", swap)
    return jnp.concatenate([chip, held, other], axis=1), cover


def etp_reduce(part, split_count, cover_near=None, cover_far=None):
    swap, _, backward = etp_perms(split_count)

    def send(value, perm):
        return lax.ppermute(value.astype(jnp.bfloat16), "etp", perm).astype(jnp.float32)

    held = part[2:5] + send(part[5:8], swap)
    arrived = send(held[2], backward)
    arrived, cover_near = lax.optimization_barrier((arrived, cover_near))
    near = held[0] + arrived
    arrived = send(jnp.stack([near, held[1]], axis=0), backward)
    arrived, cover_far = lax.optimization_barrier((arrived, cover_far))
    chip = part[0:2] + arrived
    return chip[0] + send(chip[1], swap), cover_near, cover_far


def shards(tokens, out_grad, routes, combine_weights, w_gate, w_up, w_down):
    expert_count = lax.axis_size("expert")
    split_count = lax.axis_size("etp")
    ring = split_count // 2
    me = lax.axis_index("etp")
    my_z = me // 2
    my_core = me % 2
    token_count, features = tokens.shape
    capacity = token_count // 4
    per_split = capacity // split_count
    pair_count = token_count * TOP

    flat_routes = routes.reshape(pair_count)
    expert_hot = (flat_routes[:, None] == jnp.arange(expert_count, dtype=jnp.int32)[None, :]).astype(
        jnp.int32
    )
    before = jnp.cumsum(expert_hot, axis=0) - expert_hot
    slots = jnp.sum(before * expert_hot, axis=1)

    mine = (slots // per_split) == me
    local_place = jnp.where(mine, flat_routes * per_split + slots % per_split, -1)
    place_count = expert_count * per_split
    pick = local_place[None, :] == jnp.arange(place_count, dtype=jnp.int32)[:, None]
    pick_tokens = jnp.any(pick.reshape(place_count, token_count, TOP), axis=2)

    send_rows = select_rows(pick_tokens, tokens).astype(jnp.bfloat16)
    place_weight = jnp.sum(jnp.where(pick, combine_weights.reshape(1, pair_count), 0.0), axis=1)
    send_grad = (place_weight[:, None] * select_rows(pick_tokens, out_grad)).astype(jnp.bfloat16)
    send = jnp.concatenate([send_rows, send_grad], axis=1).reshape(
        expert_count, per_split, 2 * features
    )
    recv = lax.all_to_all(send, "expert", split_axis=0, concat_axis=0, tiled=True)
    unit = recv.reshape(place_count, 2 * features)

    swap, onward, _ = etp_perms(split_count)
    weights = (w_gate[0], w_up[0], w_down[0])
    chip = jnp.stack([unit, lax.ppermute(unit, "etp", swap)], axis=0)
    first = lax.ppermute(chip, "etp", onward)
    pieces = [chip.reshape(2 * place_count, 2 * features)]
    results = [expert_rows(pieces[0][:, :features], pieces[0][:, features:], *weights)]
    first, results[0] = lax.optimization_barrier((first, results[0]))
    second = lax.ppermute(first[0], "etp", onward)
    first_other = lax.ppermute(first, "etp", swap)
    pieces.append(jnp.concatenate([first, first_other], axis=0).reshape(4 * place_count, 2 * features))
    results.append(expert_rows(pieces[1][:, :features], pieces[1][:, features:], *weights))
    second, results[1] = lax.optimization_barrier((second, results[1]))
    second_other = lax.ppermute(second, "etp", swap)
    pieces.append(jnp.concatenate([second, second_other], axis=0))
    results.append(expert_rows(pieces[2][:, :features], pieces[2][:, features:], *weights))

    rows_in = jnp.concatenate([piece[:, :features] for piece in pieces], axis=0)
    rows_grad = jnp.concatenate([piece[:, features:] for piece in pieces], axis=0)
    hidden, gate_grad, up_grad = (
        jnp.concatenate(parts, axis=0) for parts in list(zip(*results))[2:]
    )
    pair_rows = 2 * place_count
    out_part, input_part = (
        jnp.concatenate(
            [
                parts[0],
                parts[1][:pair_rows],
                parts[2][:place_count],
                parts[1][pair_rows:],
                parts[2][place_count:],
            ],
            axis=0,
        )
        for parts in list(zip(*results))[:2]
    )
    row_total = split_count * place_count

    block = (split_count, 1, place_count, features)
    sums, down_weight_grad, (gate_weight_grad, up_weight_grad) = etp_reduce(
        jnp.concatenate(
            [
                out_part.astype(jnp.bfloat16).astype(jnp.float32).reshape(block),
                input_part.astype(jnp.bfloat16).astype(jnp.float32).reshape(block),
            ],
            axis=1,
        ),
        split_count,
        contract_first(hidden, rows_grad).astype(jnp.bfloat16),
        (
            contract_first(rows_in, gate_grad).astype(jnp.bfloat16),
            contract_first(rows_in, up_grad).astype(jnp.bfloat16),
        ),
    )
    sums = sums.astype(jnp.bfloat16)
    back = jnp.concatenate(
        [
            sums[0].reshape(expert_count, per_split, features),
            sums[1].reshape(expert_count, per_split, features),
        ],
        axis=1,
    )
    back = lax.all_to_all(back, "expert", split_axis=0, concat_axis=0, tiled=True)
    back = back.reshape(expert_count, 2, per_split, features).transpose(1, 0, 2, 3)
    tables, _ = etp_gather(back.reshape(2, place_count, features), split_count)
    out_table = tables[0].reshape(row_total, features)
    input_table = tables[1].reshape(row_total, features)

    source = slots // per_split
    step = 2 * my_core - 1
    ring_offset = ((source // 2 - my_z) * step) % ring
    other_core = (source % 2) ^ my_core
    slot_of = jnp.where(
        ring_offset == 0,
        other_core,
        jnp.where(
            ring_offset == 1,
            2 + other_core,
            jnp.where(ring_offset == 2, 4 + 3 * other_core, 6 - other_core),
        ),
    )
    table_row = (slot_of * expert_count + flat_routes) * per_split + slots % per_split
    gather = table_row[:, None] == jnp.arange(row_total, dtype=jnp.int32)[None, :]
    out_pairs = select_rows(gather, out_table).reshape(token_count, TOP, features)
    input_pairs = select_rows(gather, input_table).reshape(token_count, TOP, features)
    grad_values = out_grad.astype(jnp.float32)
    mixed = jnp.sum(combine_weights[:, :, None] * out_pairs, axis=1).astype(jnp.bfloat16)
    combine_grad = jnp.sum(grad_values[:, None, :] * out_pairs, axis=2)
    tokens_grad = jnp.sum(input_pairs, axis=1).astype(jnp.bfloat16)
    return (
        mixed,
        tokens_grad,
        combine_grad,
        gate_weight_grad[None],
        up_weight_grad[None],
        down_weight_grad[None],
    )


def solution(mesh):
    return jax.shard_map(
        shards,
        mesh=mesh,
        in_specs=(
            P("expert", None),
            P("expert", None),
            P("expert", None),
            P("expert", None),
            P("expert", None, "etp"),
            P("expert", None, "etp"),
            P("expert", "etp", None),
        ),
        out_specs=(
            P("expert", None),
            P("expert", None),
            P("expert", None),
            P("expert", None, "etp"),
            P("expert", None, "etp"),
            P("expert", "etp", None),
        ),
        check_vma=False,
    )
```

profile of v0, /device:TPU:1, one launch (start us, length us, event | category | flops | bytes accessed | tf_op | source)
XLA Modules:
  0.0 150.2 jit_solution(3705155830460103966)
XLA Ops:
  6.5 17.9 %all_to_all.10 = bf16[16,4,4096]{2,1,0:T(4,128)(2,1)S(1)} all-to-all(bf16[16,4,4096]{2,1,0:T(4,128)(2,1)S(1)} %reshape.261), channel_id=1, replica_groups=mesh['expert'=16,'etp'=8] {'expert'}, dimensions={0} | all-to-all | bytes 1048576 | tf_op jit(solution)/shard_map/all_to_all | solution.py:108
  24.5 2.1 %collective-permute-start = (bf16[64,4096]{1,0:T(8,128)(2,1)S(1)}, bf16[64,4096]{1,0:T(8,128)(2,1)S(1)}, u32[]{:S(2)}, u32[]{:S(2)}) collective-permute-start(bf16[64,4096]{1,0:T(8,128)(2,1)S(1)} %reshape.262), channel_id=1, source_target_pairs={{0,1},{1,0},{2,3},{3,2},{4,5},{5,4},{6,7},{7,6},{8,9},{9,8},{10,11... | collective-permute-start | bytes 1572872 | tf_op jit(solution)/shard_map/ppermute | solution.py:113
  28.2 3.8 %collective-permute-start.1 = (bf16[2,64,4096]{2,1,0:T(8,128)(2,1)S(1)}, bf16[2,64,4096]{2,1,0:T(8,128)(2,1)S(1)}, u32[]{:S(2)}, u32[]{:S(2)}) collective-permute-start(bf16[2,64,4096]{2,1,0:T(8,128)(2,1)S(1)} %pad_maximum_fusion.4), channel_id=1, source_target_pairs={{0,2},{1,7},{2,4},{3,1},{4,6},{5,3},{6,0},{7,5},{8,10},{9,15},{10,... | collective-permute-start | bytes 3145736 | tf_op jit(solution)/shard_map/ppermute | solution.py:114
  32.0 3.5 %fusion.9 = f32[128,896]{1,0:T(8,128)S(1)} fusion(bf16[1,896,2048]{2,1,0:T(8,128)(2,1)} %param.13, bf16[128,4096]{1,0:T(8,128)(2,1)S(1)} %bitcast.154), kind=kOutput, calls=%fused_computation.12 | convolution fusion | flops 469762048 | bytes 4653056 | tf_op jit(solution)/shard_map/dot_general | solution.py:10
  43.8 1.7 %collective-permute-start.3 = (bf16[2,64,4096]{2,1,0:T(8,128)(2,1)S(1)}, bf16[2,64,4096]{2,1,0:T(8,128)(2,1)S(1)}, u32[]{:S(2)}, u32[]{:S(2)}) collective-permute-start(bf16[2,64,4096]{2,1,0:T(8,128)(2,1)S(1)} %collective-permute-done.1), channel_id=1, source_target_pairs={{0,1},{1,0},{2,3},{3,2},{4,5},{5,4},{6,7},{7,6},{8,9},{9,8},{10,11... | collective-permute-start | bytes 3145736 | tf_op jit(solution)/shard_map/ppermute | solution.py:119
  45.5 2.0 %collective-permute-start.2 = (bf16[64,4096]{1,0:T(8,128)(2,1)S(1)}, bf16[64,4096]{1,0:T(8,128)(2,1)S(1)}, u32[]{:S(2)}, u32[]{:S(2)}) collective-permute-start(bf16[64,4096]{1,0:T(8,128)(2,1)S(1)} %slice_bitcast_fusion.4), channel_id=1, source_target_pairs={{0,2},{1,7},{2,4},{3,1},{4,6},{5,3},{6,0},{7,5},{8,10},{9,15},{10,... | collective-permute-start | bytes 1572872 | tf_op jit(solution)/shard_map/ppermute | solution.py:118
  50.5 1.6 %multiply_convert_fusion.1 = (bf16[256,896]{1,0:T(8,128)(2,1)S(1)}, bf16[256,896]{1,0:T(8,128)(2,1)S(1)}, bf16[256,896]{1,0:T(8,128)(2,1)S(1)}) fusion(f32[256,896]{1,0:T(8,128)S(1)} %fusion.5, f32[256,896]{1,0:T(8,128)S(1)} %fusion.19, bf16[1,2048,896]{2,1,0:T(8,128)(2,1)S(1)} %copy-done.4, bf16[256,4096]{1,0:T(8,128)(2,1)S(1)} %bitcast.160), kind=kOutput, calls=%fused_computation.91 | convolution fusion | flops 942964736 | bytes 7929856 | tf_op jit(solution)/shard_map/dot_general | solution.py:26
  66.1 2.3 %collective-permute-done.5 = bf16[3,2,64,2048]{3,2,0,1:T(8,128)(2,1)S(1)} collective-permute-done((bf16[3,2,64,2048]{3,2,0,1:T(8,128)(2,1)S(1)}, bf16[3,2,64,2048]{3,2,0,1:T(8,128)(2,1)S(1)}, u32[]{:S(2)}, u32[]{:S(2)}) %collective-permute-start.5) | collective-permute-done | bytes 1572896 | tf_op jit(solution)/shard_map/ppermute | solution.py:65
  69.4 4.0 %convolution_convert_fusion.2 = bf16[896,2048]{1,0:T(8,128)(2,1)} fusion(bf16[128,2048]{1,0:T(8,128)(2,1)S(1)} %get-tuple-element.58, bf16[256,2048]{1,0:T(8,128)(2,1)S(1)} %get-tuple-element.47, bf16[128,2048]{1,0:T(8,128)(2,1)S(1)} %get-tuple-element.56, bf16[128,896]{1,0:T(8,128)(2,1)S(1)} %get-tuple-element.61, ...), kind=kOutput, calls=%fused_computation.42 | convolution fusion | flops 1889927168 | bytes 6684672 | tf_op jit(solution)/shard_map/dot_general | solution.py:16
  73.4 5.2 %collective-permute-done.6 = bf16[2,64,2048]{2,1,0:T(8,128)(2,1)S(1)} collective-permute-done((bf16[2,64,2048]{2,1,0:T(8,128)(2,1)S(1)}, bf16[2,64,2048]{2,1,0:T(8,128)(2,1)S(1)}, u32[]{:S(2)}, u32[]{:S(2)}) %collective-permute-start.6) | collective-permute-done | bytes 524320 | tf_op jit(solution)/shard_map/ppermute | solution.py:65
  79.0 4.2 %convolution_convert_fusion.1 = bf16[2048,896]{1,0:T(8,128)(2,1)} fusion(bf16[128,896]{1,0:T(8,128)(2,1)S(1)} %get-tuple-element.59, bf16[256,896]{1,0:T(8,128)(2,1)S(1)} %get-tuple-element.33, bf16[128,896]{1,0:T(8,128)(2,1)S(1)} %get-tuple-element.32, bf16[128,2048]{1,0:T(8,128)(2,1)S(1)} %get-tuple-element.57, ...), kind=kOutput, calls=%fused_computation.41 | convolution fusion | flops 1889927168 | bytes 6684672 | tf_op jit(solution)/shard_map/dot_general | solution.py:16
  83.2 4.2 %convolution_convert_fusion = bf16[2048,896]{1,0:T(8,128)(2,1)} fusion(bf16[128,896]{1,0:T(8,128)(2,1)S(1)} %get-tuple-element.60, bf16[256,896]{1,0:T(8,128)(2,1)S(1)} %get-tuple-element.35, bf16[128,896]{1,0:T(8,128)(2,1)S(1)} %get-tuple-element.34, bf16[128,2048]{1,0:T(8,128)(2,1)S(1)} %get-tuple-element.57, ...), kind=kOutput, calls=%fused_computation.40 | convolution fusion | flops 1889927168 | bytes 6684672 | tf_op jit(solution)/shard_map/dot_general | solution.py:16
  87.5 6.4 %collective-permute-done.7 = bf16[2,2,64,2048]{3,2,0,1:T(8,128)(2,1)S(1)} collective-permute-done((bf16[2,2,64,2048]{3,2,0,1:T(8,128)(2,1)S(1)}, bf16[2,2,64,2048]{3,2,0,1:T(8,128)(2,1)S(1)}, u32[]{:S(2)}, u32[]{:S(2)}) %collective-permute-start.7) | collective-permute-done | bytes 1048608 | tf_op jit(solution)/shard_map/ppermute | solution.py:65
  95.5 1.5 %collective-permute-done.8 = bf16[2,64,2048]{2,1,0:T(8,128)(2,1)S(1)} collective-permute-done((bf16[2,64,2048]{2,1,0:T(8,128)(2,1)S(1)}, bf16[2,64,2048]{2,1,0:T(8,128)(2,1)S(1)}, u32[]{:S(2)}, u32[]{:S(2)}) %collective-permute-start.8) | collective-permute-done | bytes 524320 | tf_op jit(solution)/shard_map/ppermute | solution.py:65
  97.7 13.4 %all_to_all.11 = bf16[16,8,2048]{2,1,0:T(8,128)(2,1)S(1)} all-to-all(bf16[16,8,2048]{2,1,0:T(8,128)(2,1)S(1)} %pad_maximum_fusion.10), channel_id=1, replica_groups=mesh['expert'=16,'etp'=8] {'expert'}, dimensions={0} | all-to-all | bytes 1048576 | tf_op jit(solution)/shard_map/all_to_all | solution.py:172
  111.7 1.9 %collective-permute-start.9 = (bf16[2,64,2048]{2,1,0:T(8,128)(2,1)S(1)}, bf16[2,64,2048]{2,1,0:T(8,128)(2,1)S(1)}, u32[]{:S(2)}, u32[]{:S(2)}) collective-permute-start(bf16[2,64,2048]{2,1,0:T(8,128)(2,1)S(1)} %reshape.266), channel_id=1, source_target_pairs={{0,1},{1,0},{2,3},{3,2},{4,5},{5,4},{6,7},{7,6},{8,9},{9,8},{10,11... | collective-permute-start | bytes 1572872 | tf_op jit(solution)/shard_map/ppermute | solution.py:51
  115.2 3.5 %collective-permute-start.10 = (bf16[2,2,64,2048]{3,2,0,1:T(8,128)(2,1)S(1)}, bf16[2,2,64,2048]{3,2,0,1:T(8,128)(2,1)S(1)}, u32[]{:S(2)}, u32[]{:S(2)}) collective-permute-start(bf16[2,2,64,2048]{3,2,0,1:T(8,128)(2,1)S(1)} %pad_maximum_fusion.6), channel_id=1, source_target_pairs={{0,2},{1,7},{2,4},{3,1},{4,6},{5,3},{6,0},{7,5},{8,10},{9,15},{10,... | collective-permute-start | bytes 3145736 | tf_op jit(solution)/shard_map/ppermute | solution.py:52
  118.7 11.7 %collective-permute-done.10 = bf16[2,2,64,2048]{3,2,0,1:T(8,128)(2,1)S(1)} collective-permute-done((bf16[2,2,64,2048]{3,2,0,1:T(8,128)(2,1)S(1)}, bf16[2,2,64,2048]{3,2,0,1:T(8,128)(2,1)S(1)}, u32[]{:S(2)}, u32[]{:S(2)}) %collective-permute-start.10) | collective-permute-done | bytes 1048608 | tf_op jit(solution)/shard_map/ppermute | solution.py:52
  130.4 3.4 %collective-permute-start.11 = (bf16[2,64,2048]{2,1,0:T(8,128)(2,1)S(1)}, bf16[2,64,2048]{2,1,0:T(8,128)(2,1)S(1)}, u32[]{:S(2)}, u32[]{:S(2)}) collective-permute-start(bf16[2,64,2048]{2,1,0:T(8,128)(2,1)S(1)} %slice_bitcast_fusion.2), channel_id=1, source_target_pairs={{0,2},{1,7},{2,4},{3,1},{4,6},{5,3},{6,0},{7,5},{8,10},{9,15},{10,... | collective-permute-start | bytes 1572872 | tf_op jit(solution)/shard_map/ppermute | solution.py:55
  134.1 5.9 %collective-permute-done.11 = bf16[2,64,2048]{2,1,0:T(8,128)(2,1)S(1)} collective-permute-done((bf16[2,64,2048]{2,1,0:T(8,128)(2,1)S(1)}, bf16[2,64,2048]{2,1,0:T(8,128)(2,1)S(1)}, u32[]{:S(2)}, u32[]{:S(2)}) %collective-permute-start.11) | collective-permute-done | bytes 524320 | tf_op jit(solution)/shard_map/ppermute | solution.py:55
  140.2 2.9 %collective-permute-start.12 = (bf16[2,3,64,2048]{3,2,1,0:T(8,128)(2,1)S(1)}, bf16[2,3,64,2048]{3,2,1,0:T(8,128)(2,1)S(1)}, u32[]{:S(2)}, u32[]{:S(2)}) collective-permute-start(bf16[2,3,64,2048]{3,2,1,0:T(8,128)(2,1)S(1)} %pad_maximum_fusion.3), channel_id=1, source_target_pairs={{0,1},{1,0},{2,3},{3,2},{4,5},{5,4},{6,7},{7,6},{8,9},{9,8},{10,11... | collective-permute-start | bytes 4718600 | tf_op jit(solution)/shard_map/ppermute | solution.py:57
  143.2 2.9 %collective-permute-done.12 = bf16[2,3,64,2048]{3,2,1,0:T(8,128)(2,1)S(1)} collective-permute-done((bf16[2,3,64,2048]{3,2,1,0:T(8,128)(2,1)S(1)}, bf16[2,3,64,2048]{3,2,1,0:T(8,128)(2,1)S(1)}, u32[]{:S(2)}, u32[]{:S(2)}) %collective-permute-start.12) | collective-permute-done | bytes 1572896 | tf_op jit(solution)/shard_map/ppermute | solution.py:57
  146.8 1.6 %convolution_reduce_fusion = bf16[128,2048]{1,0:T(8,128)(2,1)} fusion(bf16[512,2048,1]{1,0,2:T(8,128)(2,1)S(1)} %bitcast.167, s32[128,2]{0,1:T(2,128)S(1)} %get-tuple-element.67), kind=kOutput, calls=%fused_computation.64 | convolution fusion | flops 537264128 | bytes 2622464 | tf_op jit(solution)/shard_map/dot_general | solution.py:22
  148.4 1.8 %multiply_reduce_fusion = (f32[128,2]{0,1:T(2,128)}, bf16[128,2048]{1,0:T(8,128)(2,1)}) fusion(f32[128,2048]{1,0:T(8,128)S(1)} %convert_element_type.154, f32[128,2]{0,1:T(2,128)S(1)} %copy-done.6, bf16[512,2048,1]{1,0,2:T(8,128)(2,1)S(1)} %bitcast.166, s32[128,2]{0,1:T(2,128)S(1)} %get-tuple-element.67), kind=kOutput, calls=%fused_computation.60 | convolution fusion | flops 538836736 | bytes 3673088 | tf_op jit(solution)/shard_map/dot_general | solution.py:22
  (110 shorter events, 39.7 us)
Async XLA Ops:
  0.6 4.1 %copy-start = (bf16[128,2048]{1,0:T(8,128)(2,1)S(1)}, bf16[128,2048]{1,0:T(8,128)(2,1)}, u32[]{:S(2)}) copy-start(bf16[128,2048]{1,0:T(8,128)(2,1)} %param.7) | copy-start | bytes 1572868
  24.5 3.6 %collective-permute-start = (bf16[64,4096]{1,0:T(8,128)(2,1)S(1)}, bf16[64,4096]{1,0:T(8,128)(2,1)S(1)}, u32[]{:S(2)}, u32[]{:S(2)}) collective-permute-start(bf16[64,4096]{1,0:T(8,128)(2,1)S(1)} %reshape.262), channel_id=1, source_target_pairs={{0,1},{1,0},{2,3},{3,2},{4,5},{5,4},{6,7},{7,6},{8,9},{9,8},{10,11... | collective-permute-start | bytes 1572872 | tf_op jit(solution)/shard_map/ppermute | solution.py:113
  28.2 15.6 %collective-permute-start.1 = (bf16[2,64,4096]{2,1,0:T(8,128)(2,1)S(1)}, bf16[2,64,4096]{2,1,0:T(8,128)(2,1)S(1)}, u32[]{:S(2)}, u32[]{:S(2)}) collective-permute-start(bf16[2,64,4096]{2,1,0:T(8,128)(2,1)S(1)} %pad_maximum_fusion.4), channel_id=1, source_target_pairs={{0,2},{1,7},{2,4},{3,1},{4,6},{5,3},{6,0},{7,5},{8,10},{9,15},{10,... | collective-permute-start | bytes 3145736 | tf_op jit(solution)/shard_map/ppermute | solution.py:114
  32.0 3.5 %copy-start.2 = (bf16[1,2048,896]{2,1,0:T(8,128)(2,1)S(1)}, bf16[1,2048,896]{2,1,0:T(8,128)(2,1)}, u32[]{:S(2)}) copy-start(bf16[1,2048,896]{2,1,0:T(8,128)(2,1)} %param.12) | copy-start | bytes 11010052
  35.5 2.0 %copy-start.4 = (bf16[1,2048,896]{2,1,0:T(8,128)(2,1)S(1)}, bf16[1,2048,896]{2,1,0:T(8,128)(2,1)}, u32[]{:S(2)}) copy-start(bf16[1,2048,896]{2,1,0:T(8,128)(2,1)} %param.11) | copy-start | bytes 11010052
  37.6 2.0 %copy-start.3 = (bf16[1,896,2048]{2,1,0:T(8,128)(2,1)S(1)}, bf16[1,896,2048]{2,1,0:T(8,128)(2,1)}, u32[]{:S(2)}) copy-start(bf16[1,896,2048]{2,1,0:T(8,128)(2,1)} %param.13) | copy-start | bytes 11010052
  43.8 4.0 %collective-permute-start.3 = (bf16[2,64,4096]{2,1,0:T(8,128)(2,1)S(1)}, bf16[2,64,4096]{2,1,0:T(8,128)(2,1)S(1)}, u32[]{:S(2)}, u32[]{:S(2)}) collective-permute-start(bf16[2,64,4096]{2,1,0:T(8,128)(2,1)S(1)} %collective-permute-done.1), channel_id=1, source_target_pairs={{0,1},{1,0},{2,3},{3,2},{4,5},{5,4},{6,7},{7,6},{8,9},{9,8},{10,11... | collective-permute-start | bytes 3145736 | tf_op jit(solution)/shard_map/ppermute | solution.py:119
  45.5 10.5 %collective-permute-start.2 = (bf16[64,4096]{1,0:T(8,128)(2,1)S(1)}, bf16[64,4096]{1,0:T(8,128)(2,1)S(1)}, u32[]{:S(2)}, u32[]{:S(2)}) collective-permute-start(bf16[64,4096]{1,0:T(8,128)(2,1)S(1)} %slice_bitcast_fusion.4), channel_id=1, source_target_pairs={{0,2},{1,7},{2,4},{3,1},{4,6},{5,3},{6,0},{7,5},{8,10},{9,15},{10,... | collective-permute-start | bytes 1572872 | tf_op jit(solution)/shard_map/ppermute | solution.py:118
  56.0 2.0 %collective-permute-start.4 = (bf16[64,4096]{1,0:T(8,128)(2,1)S(1)}, bf16[64,4096]{1,0:T(8,128)(2,1)S(1)}, u32[]{:S(2)}, u32[]{:S(2)}) collective-permute-start(bf16[64,4096]{1,0:T(8,128)(2,1)S(1)} %collective-permute-done.2), channel_id=1, source_target_pairs={{0,1},{1,0},{2,3},{3,2},{4,5},{5,4},{6,7},{7,6},{8,9},{9,8},{10,11... | collective-permute-start | bytes 1572872 | tf_op jit(solution)/shard_map/ppermute | solution.py:123
  64.7 3.7 %collective-permute-start.5 = (bf16[3,2,64,2048]{3,2,0,1:T(8,128)(2,1)S(1)}, bf16[3,2,64,2048]{3,2,0,1:T(8,128)(2,1)S(1)}, u32[]{:S(2)}, u32[]{:S(2)}) collective-permute-start(bf16[3,2,64,2048]{3,2,0,1:T(8,128)(2,1)S(1)} %fusion.58), channel_id=1, source_target_pairs={{0,1},{1,0},{2,3},{3,2},{4,5},{5,4},{6,7},{7,6},{8,9},{9,8},{10,11... | collective-permute-start | bytes 4718600 | tf_op jit(solution)/shard_map/ppermute | solution.py:65
  69.3 9.3 %collective-permute-start.6 = (bf16[2,64,2048]{2,1,0:T(8,128)(2,1)S(1)}, bf16[2,64,2048]{2,1,0:T(8,128)(2,1)S(1)}, u32[]{:S(2)}, u32[]{:S(2)}) collective-permute-start(bf16[2,64,2048]{2,1,0:T(8,128)(2,1)S(1)} %get-tuple-element.51), channel_id=1, source_target_pairs={{2,0},{7,1},{4,2},{1,3},{6,4},{3,5},{0,6},{5,7},{10,8},{15,9},{12,... | collective-permute-start | bytes 1572872 | tf_op jit(solution)/shard_map/ppermute | solution.py:65
  78.9 14.9 %collective-permute-start.7 = (bf16[2,2,64,2048]{3,2,0,1:T(8,128)(2,1)S(1)}, bf16[2,2,64,2048]{3,2,0,1:T(8,128)(2,1)S(1)}, u32[]{:S(2)}, u32[]{:S(2)}) collective-permute-start(bf16[2,2,64,2048]{3,2,0,1:T(8,128)(2,1)S(1)} %pad_maximum_fusion.5), channel_id=1, source_target_pairs={{2,0},{7,1},{4,2},{1,3},{6,4},{3,5},{0,6},{5,7},{10,8},{15,9},{12,... | collective-permute-start | bytes 3145736 | tf_op jit(solution)/shard_map/ppermute | solution.py:65
  94.4 2.6 %collective-permute-start.8 = (bf16[2,64,2048]{2,1,0:T(8,128)(2,1)S(1)}, bf16[2,64,2048]{2,1,0:T(8,128)(2,1)S(1)}, u32[]{:S(2)}, u32[]{:S(2)}) collective-permute-start(bf16[2,64,2048]{2,1,0:T(8,128)(2,1)S(1)} %fusion.80), channel_id=1, source_target_pairs={{0,1},{1,0},{2,3},{3,2},{4,5},{5,4},{6,7},{7,6},{8,9},{9,8},{10,11... | collective-permute-start | bytes 1572872 | tf_op jit(solution)/shard_map/ppermute | solution.py:65
  111.7 3.4 %collective-permute-start.9 = (bf16[2,64,2048]{2,1,0:T(8,128)(2,1)S(1)}, bf16[2,64,2048]{2,1,0:T(8,128)(2,1)S(1)}, u32[]{:S(2)}, u32[]{:S(2)}) collective-permute-start(bf16[2,64,2048]{2,1,0:T(8,128)(2,1)S(1)} %reshape.266), channel_id=1, source_target_pairs={{0,1},{1,0},{2,3},{3,2},{4,5},{5,4},{6,7},{7,6},{8,9},{9,8},{10,11... | collective-permute-start | bytes 1572872 | tf_op jit(solution)/shard_map/ppermute | solution.py:51
  115.2 15.2 %collective-permute-start.10 = (bf16[2,2,64,2048]{3,2,0,1:T(8,128)(2,1)S(1)}, bf16[2,2,64,2048]{3,2,0,1:T(8,128)(2,1)S(1)}, u32[]{:S(2)}, u32[]{:S(2)}) collective-permute-start(bf16[2,2,64,2048]{3,2,0,1:T(8,128)(2,1)S(1)} %pad_maximum_fusion.6), channel_id=1, source_target_pairs={{0,2},{1,7},{2,4},{3,1},{4,6},{5,3},{6,0},{7,5},{8,10},{9,15},{10,... | collective-permute-start | bytes 3145736 | tf_op jit(solution)/shard_map/ppermute | solution.py:52
  130.4 9.6 %collective-permute-start.11 = (bf16[2,64,2048]{2,1,0:T(8,128)(2,1)S(1)}, bf16[2,64,2048]{2,1,0:T(8,128)(2,1)S(1)}, u32[]{:S(2)}, u32[]{:S(2)}) collective-permute-start(bf16[2,64,2048]{2,1,0:T(8,128)(2,1)S(1)} %slice_bitcast_fusion.2), channel_id=1, source_target_pairs={{0,2},{1,7},{2,4},{3,1},{4,6},{5,3},{6,0},{7,5},{8,10},{9,15},{10,... | collective-permute-start | bytes 1572872 | tf_op jit(solution)/shard_map/ppermute | solution.py:55
  134.1 8.9 %copy-start.5 = (bf16[128,2048]{1,0:T(8,128)(2,1)S(1)}, bf16[128,2048]{1,0:T(8,128)(2,1)}, u32[]{:S(2)}) copy-start(bf16[128,2048]{1,0:T(8,128)(2,1)} %param.8) | copy-start | bytes 1572868
  140.2 6.0 %collective-permute-start.12 = (bf16[2,3,64,2048]{3,2,1,0:T(8,128)(2,1)S(1)}, bf16[2,3,64,2048]{3,2,1,0:T(8,128)(2,1)S(1)}, u32[]{:S(2)}, u32[]{:S(2)}) collective-permute-start(bf16[2,3,64,2048]{3,2,1,0:T(8,128)(2,1)S(1)} %pad_maximum_fusion.3), channel_id=1, source_target_pairs={{0,1},{1,0},{2,3},{3,2},{4,5},{5,4},{6,7},{7,6},{8,9},{9,8},{10,11... | collective-permute-start | bytes 4718600 | tf_op jit(solution)/shard_map/ppermute | solution.py:57
  146.8 1.6 %copy-start.6 = (f32[128,2]{0,1:T(2,128)S(1)}, f32[128,2]{0,1:T(2,128)}, u32[]{:S(2)}) copy-start(f32[128,2]{0,1:T(2,128)} %param.10) | copy-start | bytes 3076
  148.4 1.8 %copy-start.1 = (bf16[128,2048]{1,0:T(8,128)(2,1)S(1)}, bf16[128,2048]{1,0:T(8,128)(2,1)}, u32[]{:S(2)}) copy-start(bf16[128,2048]{1,0:T(8,128)(2,1)} %param.7) | copy-start | bytes 1572868
where the time goes:
time: 151 us; the launch traced here: 150 us
  waiting for transfers between devices  41 us (27%)
  matrix products  40 us (26%)
  blocking collectives  31.3 us (21%)
  starting transfers between devices  23.6 us (16%)
  local copies, waits for them, and re-layouts  8.18 us (5%)
  other arithmetic  4.91 us (3%)
    all_to_all x1, blocking collectives, shards(): lax.all_to_all(send, 'expert', split_axis=0, concat_axis=0, tiled=True)  17.9 us
    ppermute x4, waiting for transfers between devices, send(): lax.ppermute(value.astype(jnp.bfloat16), 'etp', perm).astype(jnp.float32)  15.4 us
    dot_general x9, matrix products, contract_last(): lax.dot_general(left, right, (((1,), (1,)), ((), ())), preferred_element_...  13.9 us
    all_to_all x1, blocking collectives, shards(): lax.all_to_all(back, 'expert', split_axis=0, concat_axis=0, tiled=True)  13.4 us
    dot_general x3, matrix products, contract_first(): lax.dot_general(left, right, (((0,), (0,)), ((), ())), preferred_element_...  12.4 us
    ppermute x1, waiting for transfers between devices, etp_gather(): first = lax.ppermute(chip, 'etp', onward)  11.7 us
    ppermute x1, waiting for transfers between devices, etp_gather(): second = lax.ppermute(first[:, 0], 'etp', onward)  5.86 us
    dot_general x4, matrix products, select_rows(): jnp.dot(selector.astype(table.dtype), table, preferred_element_type=jnp.f...  4.91 us
  transfers between devices with their start and end apart: 13, of which 12 were waited for; matrix products, arithmetic and copies ran while one was open for 21% of the time, Pallas kernels for 0%

commit v1 on v0

--- a/solution.py
+++ b/solution.py
@@ -53,9 +53,11 @@
     if cover is not None:
         first, cover = lax.optimization_barrier((first, cover))
     second = lax.ppermute(first[:, 0], "etp", onward)
-    held = jnp.concatenate([first, second[:, None]], axis=1)
-    other = lax.ppermute(held, "etp", swap)
-    return jnp.concatenate([chip, held, other], axis=1), cover
+    first_other = lax.ppermute(first, "etp", swap)
+    second_other = lax.ppermute(second, "etp", swap)
+    return jnp.concatenate(
+        [chip, first, second[:, None], first_other, second_other[:, None]], axis=1
+    ), cover
 
 
 def etp_reduce(part, split_count, cover_near=None, cover_far=None):

time: 151 us -> 149 us (0.987)
    ppermute x1 -> x2, waiting for transfers between devices: 2.89 us -> 1.38 us  [the longest x1 1.37 us: etp_gather(): second_other = lax.ppermute(second, 'etp', swap)]
    unnamed x27 -> x29, local copies, waits for them, and re-layouts: 4.52 us -> 4.7 us
  transfers between devices with their start and end apart: 13 -> 14, of which waited for: 12 -> 12; matrix products, arithmetic and copies ran while one was open for 21% -> 21% of each run, Pallas kernels for 0% -> 0%
where the time goes in v1:
time: 149 us; the launch traced here: 148 us
  matrix products  39.8 us (27%)
  waiting for transfers between devices  39.7 us (27%)
  blocking collectives  31.3 us (21%)
  starting transfers between devices  23.5 us (16%)
  local copies, waits for them, and re-layouts  8.04 us (5%)
  other arithmetic  4.77 us (3%)
    all_to_all x1, blocking collectives, shards(): lax.all_to_all(send, 'expert', split_axis=0, concat_axis=0, tiled=True)  17.9 us
    ppermute x4, waiting for transfers between devices, send(): lax.ppermute(value.astype(jnp.bfloat16), 'etp', perm).astype(jnp.float32)  15.3 us
    dot_general x9, matrix products, contract_last(): lax.dot_general(left, right, (((1,), (1,)), ((), ())), preferred_element_...  13.7 us
    all_to_all x1, blocking collectives, shards(): lax.all_to_all(back, 'expert', split_axis=0, concat_axis=0, tiled=True)  13.4 us
    dot_general x3, matrix products, contract_first(): lax.dot_general(left, right, (((0,), (0,)), ((), ())), preferred_element_...  12.4 us
    ppermute x1, waiting for transfers between devices, etp_gather(): first = lax.ppermute(chip, 'etp', onward)  11.6 us
    ppermute x1, waiting for transfers between devices, etp_gather(): second = lax.ppermute(first[:, 0], 'etp', onward)  6.01 us
    dot_general x4, matrix products, select_rows(): jnp.dot(selector.astype(table.dtype), table, preferred_element_type=jnp.f...  4.91 us
  transfers between devices with their start and end apart: 14, of which 12 were waited for; matrix products, arithmetic and copies ran while one was open for 21% of the time, Pallas kernels for 0%

profile of v1, /device:TPU:1, one launch (start us, length us, event | category | flops | bytes accessed | tf_op | source)
XLA Modules:
  0.0 148.5 jit_solution(2916250335875788779)
XLA Ops:
  6.5 17.9 %all_to_all.10 = bf16[16,4,4096]{2,1,0:T(4,128)(2,1)S(1)} all-to-all(bf16[16,4,4096]{2,1,0:T(4,128)(2,1)S(1)} %reshape.261), channel_id=1, replica_groups=mesh['expert'=16,'etp'=8] {'expert'}, dimensions={0} | all-to-all | bytes 1048576 | tf_op jit(solution)/shard_map/all_to_all | solution.py:110
  24.5 2.1 %collective-permute-start = (bf16[64,4096]{1,0:T(8,128)(2,1)S(1)}, bf16[64,4096]{1,0:T(8,128)(2,1)S(1)}, u32[]{:S(2)}, u32[]{:S(2)}) collective-permute-start(bf16[64,4096]{1,0:T(8,128)(2,1)S(1)} %reshape.262), channel_id=1, source_target_pairs={{0,1},{1,0},{2,3},{3,2},{4,5},{5,4},{6,7},{7,6},{8,9},{9,8},{10,11... | collective-permute-start | bytes 1572872 | tf_op jit(solution)/shard_map/ppermute | solution.py:115
  28.2 3.8 %collective-permute-start.1 = (bf16[2,64,4096]{2,1,0:T(8,128)(2,1)S(1)}, bf16[2,64,4096]{2,1,0:T(8,128)(2,1)S(1)}, u32[]{:S(2)}, u32[]{:S(2)}) collective-permute-start(bf16[2,64,4096]{2,1,0:T(8,128)(2,1)S(1)} %pad_maximum_fusion.3), channel_id=1, source_target_pairs={{0,2},{1,7},{2,4},{3,1},{4,6},{5,3},{6,0},{7,5},{8,10},{9,15},{10,... | collective-permute-start | bytes 3145736 | tf_op jit(solution)/shard_map/ppermute | solution.py:116
  32.0 3.3 %fusion.9 = f32[128,896]{1,0:T(8,128)S(1)} fusion(bf16[1,896,2048]{2,1,0:T(8,128)(2,1)} %param.13, bf16[128,4096]{1,0:T(8,128)(2,1)S(1)} %bitcast.158), kind=kOutput, calls=%fused_computation.12 | convolution fusion | flops 469762048 | bytes 4653056 | tf_op jit(solution)/shard_map/dot_general | solution.py:10
  43.8 1.7 %collective-permute-start.3 = (bf16[2,64,4096]{2,1,0:T(8,128)(2,1)S(1)}, bf16[2,64,4096]{2,1,0:T(8,128)(2,1)S(1)}, u32[]{:S(2)}, u32[]{:S(2)}) collective-permute-start(bf16[2,64,4096]{2,1,0:T(8,128)(2,1)S(1)} %collective-permute-done.1), channel_id=1, source_target_pairs={{0,1},{1,0},{2,3},{3,2},{4,5},{5,4},{6,7},{7,6},{8,9},{9,8},{10,11... | collective-permute-start | bytes 3145736 | tf_op jit(solution)/shard_map/ppermute | solution.py:121
  45.5 2.0 %collective-permute-start.2 = (bf16[64,4096]{1,0:T(8,128)(2,1)S(1)}, bf16[64,4096]{1,0:T(8,128)(2,1)S(1)}, u32[]{:S(2)}, u32[]{:S(2)}) collective-permute-start(bf16[64,4096]{1,0:T(8,128)(2,1)S(1)} %slice_bitcast_fusion.4), channel_id=1, source_target_pairs={{0,2},{1,7},{2,4},{3,1},{4,6},{5,3},{6,0},{7,5},{8,10},{9,15},{10,... | collective-permute-start | bytes 1572872 | tf_op jit(solution)/shard_map/ppermute | solution.py:120
  50.5 1.6 %multiply_convert_fusion.1 = (bf16[256,896]{1,0:T(8,128)(2,1)S(1)}, bf16[256,896]{1,0:T(8,128)(2,1)S(1)}, bf16[256,896]{1,0:T(8,128)(2,1)S(1)}) fusion(f32[256,896]{1,0:T(8,128)S(1)} %fusion.5, f32[256,896]{1,0:T(8,128)S(1)} %fusion.19, bf16[1,2048,896]{2,1,0:T(8,128)(2,1)S(1)} %copy-done.4, bf16[256,4096]{1,0:T(8,128)(2,1)S(1)} %bitcast.164), kind=kOutput, calls=%fused_computation.92 | convolution fusion | flops 942964736 | bytes 7929856 | tf_op jit(solution)/shard_map/dot_general | solution.py:26
  66.1 2.3 %collective-permute-done.5 = bf16[3,2,64,2048]{3,2,0,1:T(8,128)(2,1)S(1)} collective-permute-done((bf16[3,2,64,2048]{3,2,0,1:T(8,128)(2,1)S(1)}, bf16[3,2,64,2048]{3,2,0,1:T(8,128)(2,1)S(1)}, u32[]{:S(2)}, u32[]{:S(2)}) %collective-permute-start.5) | collective-permute-done | bytes 1572896 | tf_op jit(solution)/shard_map/ppermute | solution.py:67
  69.4 4.0 %convolution_convert_fusion.2 = bf16[896,2048]{1,0:T(8,128)(2,1)} fusion(bf16[128,2048]{1,0:T(8,128)(2,1)S(1)} %get-tuple-element.56, bf16[256,2048]{1,0:T(8,128)(2,1)S(1)} %get-tuple-element.47, bf16[128,2048]{1,0:T(8,128)(2,1)S(1)} %get-tuple-element.54, bf16[128,896]{1,0:T(8,128)(2,1)S(1)} %get-tuple-element.59, ...), kind=kOutput, calls=%fused_computation.42 | convolution fusion | flops 1889927168 | bytes 6684672 | tf_op jit(solution)/shard_map/dot_general | solution.py:16
  73.4 5.2 %collective-permute-done.6 = bf16[2,64,2048]{2,1,0:T(8,128)(2,1)S(1)} collective-permute-done((bf16[2,64,2048]{2,1,0:T(8,128)(2,1)S(1)}, bf16[2,64,2048]{2,1,0:T(8,128)(2,1)S(1)}, u32[]{:S(2)}, u32[]{:S(2)}) %collective-permute-start.6) | collective-permute-done | bytes 524320 | tf_op jit(solution)/shard_map/ppermute | solution.py:67
  79.0 4.2 %convolution_convert_fusion.1 = bf16[2048,896]{1,0:T(8,128)(2,1)} fusion(bf16[128,896]{1,0:T(8,128)(2,1)S(1)} %get-tuple-element.57, bf16[256,896]{1,0:T(8,128)(2,1)S(1)} %get-tuple-element.33, bf16[128,896]{1,0:T(8,128)(2,1)S(1)} %get-tuple-element.32, bf16[128,2048]{1,0:T(8,128)(2,1)S(1)} %get-tuple-element.55, ...), kind=kOutput, calls=%fused_computation.41 | convolution fusion | flops 1889927168 | bytes 6684672 | tf_op jit(solution)/shard_map/dot_general | solution.py:16
  83.2 4.2 %convolution_convert_fusion = bf16[2048,896]{1,0:T(8,128)(2,1)} fusion(bf16[128,896]{1,0:T(8,128)(2,1)S(1)} %get-tuple-element.58, bf16[256,896]{1,0:T(8,128)(2,1)S(1)} %get-tuple-element.35, bf16[128,896]{1,0:T(8,128)(2,1)S(1)} %get-tuple-element.34, bf16[128,2048]{1,0:T(8,128)(2,1)S(1)} %get-tuple-element.55, ...), kind=kOutput, calls=%fused_computation.40 | convolution fusion | flops 1889927168 | bytes 6684672 | tf_op jit(solution)/shard_map/dot_general | solution.py:16
  87.5 6.4 %collective-permute-done.7 = bf16[2,2,64,2048]{3,2,0,1:T(8,128)(2,1)S(1)} collective-permute-done((bf16[2,2,64,2048]{3,2,0,1:T(8,128)(2,1)S(1)}, bf16[2,2,64,2048]{3,2,0,1:T(8,128)(2,1)S(1)}, u32[]{:S(2)}, u32[]{:S(2)}) %collective-permute-start.7) | collective-permute-done | bytes 1048608 | tf_op jit(solution)/shard_map/ppermute | solution.py:67
  95.5 1.5 %collective-permute-done.8 = bf16[2,64,2048]{2,1,0:T(8,128)(2,1)S(1)} collective-permute-done((bf16[2,64,2048]{2,1,0:T(8,128)(2,1)S(1)}, bf16[2,64,2048]{2,1,0:T(8,128)(2,1)S(1)}, u32[]{:S(2)}, u32[]{:S(2)}) %collective-permute-start.8) | collective-permute-done | bytes 524320 | tf_op jit(solution)/shard_map/ppermute | solution.py:67
  97.7 13.4 %all_to_all.11 = bf16[16,8,2048]{2,1,0:T(8,128)(2,1)S(1)} all-to-all(bf16[16,8,2048]{2,1,0:T(8,128)(2,1)S(1)} %pad_maximum_fusion.9), channel_id=1, replica_groups=mesh['expert'=16,'etp'=8] {'expert'}, dimensions={0} | all-to-all | bytes 1048576 | tf_op jit(solution)/shard_map/all_to_all | solution.py:174
  111.7 1.9 %collective-permute-start.9 = (bf16[2,64,2048]{2,1,0:T(8,128)(2,1)S(1)}, bf16[2,64,2048]{2,1,0:T(8,128)(2,1)S(1)}, u32[]{:S(2)}, u32[]{:S(2)}) collective-permute-start(bf16[2,64,2048]{2,1,0:T(8,128)(2,1)S(1)} %reshape.266), channel_id=1, source_target_pairs={{0,1},{1,0},{2,3},{3,2},{4,5},{5,4},{6,7},{7,6},{8,9},{9,8},{10,11... | collective-permute-start | bytes 1572872 | tf_op jit(solution)/shard_map/ppermute | solution.py:51
  113.6 1.4 collective-permute-done.9
  115.2 3.7 %collective-permute-start.10 = (bf16[2,2,64,2048]{3,2,0,1:T(8,128)(2,1)S(1)}, bf16[2,2,64,2048]{3,2,0,1:T(8,128)(2,1)S(1)}, u32[]{:S(2)}, u32[]{:S(2)}) collective-permute-start(bf16[2,2,64,2048]{3,2,0,1:T(8,128)(2,1)S(1)} %pad_maximum_fusion.5), channel_id=1, source_target_pairs={{0,2},{1,7},{2,4},{3,1},{4,6},{5,3},{6,0},{7,5},{8,10},{9,15},{10,... | collective-permute-start | bytes 3145736 | tf_op jit(solution)/shard_map/ppermute | solution.py:52
  119.0 11.6 %collective-permute-done.10 = bf16[2,2,64,2048]{3,2,0,1:T(8,128)(2,1)S(1)} collective-permute-done((bf16[2,2,64,2048]{3,2,0,1:T(8,128)(2,1)S(1)}, bf16[2,2,64,2048]{3,2,0,1:T(8,128)(2,1)S(1)}, u32[]{:S(2)}, u32[]{:S(2)}) %collective-permute-start.10) | collective-permute-done | bytes 1048608 | tf_op jit(solution)/shard_map/ppermute | solution.py:52
  130.7 3.2 %collective-permute-start.11 = (bf16[2,64,2048]{2,1,0:T(8,128)(2,1)S(1)}, bf16[2,64,2048]{2,1,0:T(8,128)(2,1)S(1)}, u32[]{:S(2)}, u32[]{:S(2)}) collective-permute-start(bf16[2,64,2048]{2,1,0:T(8,128)(2,1)S(1)} %slice_bitcast_fusion.2), channel_id=1, source_target_pairs={{0,2},{1,7},{2,4},{3,1},{4,6},{5,3},{6,0},{7,5},{8,10},{9,15},{10,... | collective-permute-start | bytes 1572872 | tf_op jit(solution)/shard_map/ppermute | solution.py:55
  134.0 6.0 %collective-permute-done.11 = bf16[2,64,2048]{2,1,0:T(8,128)(2,1)S(1)} collective-permute-done((bf16[2,64,2048]{2,1,0:T(8,128)(2,1)S(1)}, bf16[2,64,2048]{2,1,0:T(8,128)(2,1)S(1)}, u32[]{:S(2)}, u32[]{:S(2)}) %collective-permute-start.11) | collective-permute-done | bytes 524320 | tf_op jit(solution)/shard_map/ppermute | solution.py:55
  140.0 2.8 %collective-permute-start.13 = (bf16[2,64,2048]{2,1,0:T(8,128)(2,1)S(1)}, bf16[2,64,2048]{2,1,0:T(8,128)(2,1)S(1)}, u32[]{:S(2)}, u32[]{:S(2)}) collective-permute-start(bf16[2,64,2048]{2,1,0:T(8,128)(2,1)S(1)} %collective-permute-done.11), channel_id=1, source_target_pairs={{0,1},{1,0},{2,3},{3,2},{4,5},{5,4},{6,7},{7,6},{8,9},{9,8},{10,11... | collective-permute-start | bytes 1572872 | tf_op jit(solution)/shard_map/ppermute | solution.py:57
  145.0 1.6 %convolution_reduce_fusion = bf16[128,2048]{1,0:T(8,128)(2,1)} fusion(bf16[512,2048,1]{1,0,2:T(8,128)(2,1)S(1)} %bitcast.170, s32[128,2]{0,1:T(2,128)S(1)} %get-tuple-element.65), kind=kOutput, calls=%fused_computation.63 | convolution fusion | flops 537264128 | bytes 2622464 | tf_op jit(solution)/shard_map/dot_general | solution.py:22
  146.6 1.8 %multiply_reduce_fusion = (f32[128,2]{0,1:T(2,128)}, bf16[128,2048]{1,0:T(8,128)(2,1)}) fusion(f32[128,2048]{1,0:T(8,128)S(1)} %convert_element_type.154, f32[128,2]{0,1:T(2,128)S(1)} %copy-done.6, bf16[512,2048,1]{1,0,2:T(8,128)(2,1)S(1)} %bitcast.169, s32[128,2]{0,1:T(2,128)S(1)} %get-tuple-element.65), kind=kOutput, calls=%fused_computation.60 | convolution fusion | flops 538836736 | bytes 3673088 | tf_op jit(solution)/shard_map/dot_general | solution.py:22
  (112 shorter events, 39.6 us)
Async XLA Ops:
  0.6 4.1 %copy-start = (bf16[128,2048]{1,0:T(8,128)(2,1)S(1)}, bf16[128,2048]{1,0:T(8,128)(2,1)}, u32[]{:S(2)}) copy-start(bf16[128,2048]{1,0:T(8,128)(2,1)} %param.7) | copy-start | bytes 1572868
  24.5 3.6 %collective-permute-start = (bf16[64,4096]{1,0:T(8,128)(2,1)S(1)}, bf16[64,4096]{1,0:T(8,128)(2,1)S(1)}, u32[]{:S(2)}, u32[]{:S(2)}) collective-permute-start(bf16[64,4096]{1,0:T(8,128)(2,1)S(1)} %reshape.262), channel_id=1, source_target_pairs={{0,1},{1,0},{2,3},{3,2},{4,5},{5,4},{6,7},{7,6},{8,9},{9,8},{10,11... | collective-permute-start | bytes 1572872 | tf_op jit(solution)/shard_map/ppermute | solution.py:115
  28.1 7.3 %copy-start.2 = (bf16[1,2048,896]{2,1,0:T(8,128)(2,1)S(1)}, bf16[1,2048,896]{2,1,0:T(8,128)(2,1)}, u32[]{:S(2)}) copy-start(bf16[1,2048,896]{2,1,0:T(8,128)(2,1)} %param.12) | copy-start | bytes 11010052
  28.2 15.6 %collective-permute-start.1 = (bf16[2,64,4096]{2,1,0:T(8,128)(2,1)S(1)}, bf16[2,64,4096]{2,1,0:T(8,128)(2,1)S(1)}, u32[]{:S(2)}, u32[]{:S(2)}) collective-permute-start(bf16[2,64,4096]{2,1,0:T(8,128)(2,1)S(1)} %pad_maximum_fusion.3), channel_id=1, source_target_pairs={{0,2},{1,7},{2,4},{3,1},{4,6},{5,3},{6,0},{7,5},{8,10},{9,15},{10,... | collective-permute-start | bytes 3145736 | tf_op jit(solution)/shard_map/ppermute | solution.py:116
  35.4 2.0 %copy-start.4 = (bf16[1,2048,896]{2,1,0:T(8,128)(2,1)S(1)}, bf16[1,2048,896]{2,1,0:T(8,128)(2,1)}, u32[]{:S(2)}) copy-start(bf16[1,2048,896]{2,1,0:T(8,128)(2,1)} %param.11) | copy-start | bytes 11010052
  37.4 2.0 %copy-start.3 = (bf16[1,896,2048]{2,1,0:T(8,128)(2,1)S(1)}, bf16[1,896,2048]{2,1,0:T(8,128)(2,1)}, u32[]{:S(2)}) copy-start(bf16[1,896,2048]{2,1,0:T(8,128)(2,1)} %param.13) | copy-start | bytes 11010052
  43.8 4.0 %collective-permute-start.3 = (bf16[2,64,4096]{2,1,0:T(8,128)(2,1)S(1)}, bf16[2,64,4096]{2,1,0:T(8,128)(2,1)S(1)}, u32[]{:S(2)}, u32[]{:S(2)}) collective-permute-start(bf16[2,64,4096]{2,1,0:T(8,128)(2,1)S(1)} %collective-permute-done.1), channel_id=1, source_target_pairs={{0,1},{1,0},{2,3},{3,2},{4,5},{5,4},{6,7},{7,6},{8,9},{9,8},{10,11... | collective-permute-start | bytes 3145736 | tf_op jit(solution)/shard_map/ppermute | solution.py:121
  45.5 10.5 %collective-permute-start.2 = (bf16[64,4096]{1,0:T(8,128)(2,1)S(1)}, bf16[64,4096]{1,0:T(8,128)(2,1)S(1)}, u32[]{:S(2)}, u32[]{:S(2)}) collective-permute-start(bf16[64,4096]{1,0:T(8,128)(2,1)S(1)} %slice_bitcast_fusion.4), channel_id=1, source_target_pairs={{0,2},{1,7},{2,4},{3,1},{4,6},{5,3},{6,0},{7,5},{8,10},{9,15},{10,... | collective-permute-start | bytes 1572872 | tf_op jit(solution)/shard_map/ppermute | solution.py:120
  56.0 2.0 %collective-permute-start.4 = (bf16[64,4096]{1,0:T(8,128)(2,1)S(1)}, bf16[64,4096]{1,0:T(8,128)(2,1)S(1)}, u32[]{:S(2)}, u32[]{:S(2)}) collective-permute-start(bf16[64,4096]{1,0:T(8,128)(2,1)S(1)} %collective-permute-done.2), channel_id=1, source_target_pairs={{0,1},{1,0},{2,3},{3,2},{4,5},{5,4},{6,7},{7,6},{8,9},{9,8},{10,11... | collective-permute-start | bytes 1572872 | tf_op jit(solution)/shard_map/ppermute | solution.py:125
  64.7 3.7 %collective-permute-start.5 = (bf16[3,2,64,2048]{3,2,0,1:T(8,128)(2,1)S(1)}, bf16[3,2,64,2048]{3,2,0,1:T(8,128)(2,1)S(1)}, u32[]{:S(2)}, u32[]{:S(2)}) collective-permute-start(bf16[3,2,64,2048]{3,2,0,1:T(8,128)(2,1)S(1)} %fusion.58), channel_id=1, source_target_pairs={{0,1},{1,0},{2,3},{3,2},{4,5},{5,4},{6,7},{7,6},{8,9},{9,8},{10,11... | collective-permute-start | bytes 4718600 | tf_op jit(solution)/shard_map/ppermute | solution.py:67
  69.3 9.3 %collective-permute-start.6 = (bf16[2,64,2048]{2,1,0:T(8,128)(2,1)S(1)}, bf16[2,64,2048]{2,1,0:T(8,128)(2,1)S(1)}, u32[]{:S(2)}, u32[]{:S(2)}) collective-permute-start(bf16[2,64,2048]{2,1,0:T(8,128)(2,1)S(1)} %get-tuple-element.51), channel_id=1, source_target_pairs={{2,0},{7,1},{4,2},{1,3},{6,4},{3,5},{0,6},{5,7},{10,8},{15,9},{12,... | collective-permute-start | bytes 1572872 | tf_op jit(solution)/shard_map/ppermute | solution.py:67
  78.9 14.9 %collective-permute-start.7 = (bf16[2,2,64,2048]{3,2,0,1:T(8,128)(2,1)S(1)}, bf16[2,2,64,2048]{3,2,0,1:T(8,128)(2,1)S(1)}, u32[]{:S(2)}, u32[]{:S(2)}) collective-permute-start(bf16[2,2,64,2048]{3,2,0,1:T(8,128)(2,1)S(1)} %pad_maximum_fusion.4), channel_id=1, source_target_pairs={{2,0},{7,1},{4,2},{1,3},{6,4},{3,5},{0,6},{5,7},{10,8},{15,9},{12,... | collective-permute-start | bytes 3145736 | tf_op jit(solution)/shard_map/ppermute | solution.py:67
  94.4 2.6 %collective-permute-start.8 = (bf16[2,64,2048]{2,1,0:T(8,128)(2,1)S(1)}, bf16[2,64,2048]{2,1,0:T(8,128)(2,1)S(1)}, u32[]{:S(2)}, u32[]{:S(2)}) collective-permute-start(bf16[2,64,2048]{2,1,0:T(8,128)(2,1)S(1)} %fusion.80), channel_id=1, source_target_pairs={{0,1},{1,0},{2,3},{3,2},{4,5},{5,4},{6,7},{7,6},{8,9},{9,8},{10,11... | collective-permute-start | bytes 1572872 | tf_op jit(solution)/shard_map/ppermute | solution.py:67
  111.1 7.8 %copy-start.5 = (bf16[128,2048]{1,0:T(8,128)(2,1)S(1)}, bf16[128,2048]{1,0:T(8,128)(2,1)}, u32[]{:S(2)}) copy-start(bf16[128,2048]{1,0:T(8,128)(2,1)} %param.8) | copy-start | bytes 1572868
  111.7 3.4 %collective-permute-start.9 = (bf16[2,64,2048]{2,1,0:T(8,128)(2,1)S(1)}, bf16[2,64,2048]{2,1,0:T(8,128)(2,1)S(1)}, u32[]{:S(2)}, u32[]{:S(2)}) collective-permute-start(bf16[2,64,2048]{2,1,0:T(8,128)(2,1)S(1)} %reshape.266), channel_id=1, source_target_pairs={{0,1},{1,0},{2,3},{3,2},{4,5},{5,4},{6,7},{7,6},{8,9},{9,8},{10,11... | collective-permute-start | bytes 1572872 | tf_op jit(solution)/shard_map/ppermute | solution.py:51
  115.2 15.5 %collective-permute-start.10 = (bf16[2,2,64,2048]{3,2,0,1:T(8,128)(2,1)S(1)}, bf16[2,2,64,2048]{3,2,0,1:T(8,128)(2,1)S(1)}, u32[]{:S(2)}, u32[]{:S(2)}) collective-permute-start(bf16[2,2,64,2048]{3,2,0,1:T(8,128)(2,1)S(1)} %pad_maximum_fusion.5), channel_id=1, source_target_pairs={{0,2},{1,7},{2,4},{3,1},{4,6},{5,3},{6,0},{7,5},{8,10},{9,15},{10,... | collective-permute-start | bytes 3145736 | tf_op jit(solution)/shard_map/ppermute | solution.py:52
  130.7 9.3 %collective-permute-start.11 = (bf16[2,64,2048]{2,1,0:T(8,128)(2,1)S(1)}, bf16[2,64,2048]{2,1,0:T(8,128)(2,1)S(1)}, u32[]{:S(2)}, u32[]{:S(2)}) collective-permute-start(bf16[2,64,2048]{2,1,0:T(8,128)(2,1)S(1)} %slice_bitcast_fusion.2), channel_id=1, source_target_pairs={{0,2},{1,7},{2,4},{3,1},{4,6},{5,3},{6,0},{7,5},{8,10},{9,15},{10,... | collective-permute-start | bytes 1572872 | tf_op jit(solution)/shard_map/ppermute | solution.py:55
  133.9 9.0 %collective-permute-start.12 = (bf16[2,2,64,2048]{3,2,0,1:T(8,128)(2,1)S(1)}, bf16[2,2,64,2048]{3,2,0,1:T(8,128)(2,1)S(1)}, u32[]{:S(2)}, u32[]{:S(2)}) collective-permute-start(bf16[2,2,64,2048]{3,2,0,1:T(8,128)(2,1)S(1)} %collective-permute-done.10), channel_id=1, source_target_pairs={{0,1},{1,0},{2,3},{3,2},{4,5},{5,4},{6,7},{7,6},{8,9},{9,8},{10,11... | collective-permute-start | bytes 3145736 | tf_op jit(solution)/shard_map/ppermute | solution.py:56
  140.0 4.4 %collective-permute-start.13 = (bf16[2,64,2048]{2,1,0:T(8,128)(2,1)S(1)}, bf16[2,64,2048]{2,1,0:T(8,128)(2,1)S(1)}, u32[]{:S(2)}, u32[]{:S(2)}) collective-permute-start(bf16[2,64,2048]{2,1,0:T(8,128)(2,1)S(1)} %collective-permute-done.11), channel_id=1, source_target_pairs={{0,1},{1,0},{2,3},{3,2},{4,5},{5,4},{6,7},{7,6},{8,9},{9,8},{10,11... | collective-permute-start | bytes 1572872 | tf_op jit(solution)/shard_map/ppermute | solution.py:57
  144.4 2.2 %copy-start.6 = (f32[128,2]{0,1:T(2,128)S(1)}, f32[128,2]{0,1:T(2,128)}, u32[]{:S(2)}) copy-start(f32[128,2]{0,1:T(2,128)} %param.10) | copy-start | bytes 3076
  145.0 3.4 %copy-start.1 = (bf16[128,2048]{1,0:T(8,128)(2,1)S(1)}, bf16[128,2048]{1,0:T(8,128)(2,1)}, u32[]{:S(2)}) copy-start(bf16[128,2048]{1,0:T(8,128)(2,1)} %param.7) | copy-start | bytes 1572868

commit v2 on v1

--- a/solution.py
+++ b/solution.py
@@ -66,13 +66,13 @@
     def send(value, perm):
         return lax.ppermute(value.astype(jnp.bfloat16), "etp", perm).astype(jnp.float32)
 
-    held = part[2:5] + send(part[5:8], swap)
-    arrived = send(held[2], backward)
+    pair = send(jnp.stack([part[5], part[6]], axis=0), swap)
+    arrived = send(part[4] + send(part[7], swap), backward)
     arrived, cover_near = lax.optimization_barrier((arrived, cover_near))
-    near = held[0] + arrived
-    arrived = send(jnp.stack([near, held[1]], axis=0), backward)
+    near = part[2] + pair[0] + arrived
+    arrived = send(jnp.stack([near, part[3] + pair[1]], axis=0), backward)
     arrived, cover_far = lax.optimization_barrier((arrived, cover_far))
-    chip = part[0:2] + arrived
+    chip = jnp.stack([part[0], part[1]], axis=0) + arrived
     return chip[0] + send(chip[1], swap), cover_near, cover_far
 
 
@@ -131,31 +131,22 @@
     hidden, gate_grad, up_grad = (
         jnp.concatenate(parts, axis=0) for parts in list(zip(*results))[2:]
     )
-    pair_rows = 2 * place_count
-    out_part, input_part = (
-        jnp.concatenate(
-            [
-                parts[0],
-                parts[1][:pair_rows],
-                parts[2][:place_count],
-                parts[1][pair_rows:],
-                parts[2][place_count:],
-            ],
-            axis=0,
-        )
-        for parts in list(zip(*results))[:2]
-    )
+    chunk_slots = ((0, 1), (2, 3, 5, 6), (4, 7))
+    part = [None] * split_count
+    for slots_of_chunk, result in zip(chunk_slots, results):
+        for index, slot in enumerate(slots_of_chunk):
+            rows = slice(index * place_count, (index + 1) * place_count)
+            part[slot] = jnp.stack(
+                [
+                    result[0][rows].astype(jnp.bfloat16).astype(jnp.float32),
+                    result[1][rows].astype(jnp.bfloat16).astype(jnp.float32),
+                ],
+                axis=0,
+            )
     row_total = split_count * place_count
 
-    block = (split_count, 1, place_count, features)
     sums, down_weight_grad, (gate_weight_grad, up_weight_grad) = etp_reduce(
-        jnp.concatenate(
-            [
-                out_part.astype(jnp.bfloat16).astype(jnp.float32).reshape(block),
-                input_part.astype(jnp.bfloat16).astype(jnp.float32).reshape(block),
-            ],
-            axis=1,
-        ),
+        part,
         split_count,
         contract_first(hidden, rows_grad).astype(jnp.bfloat16),
         (

time: 149 us -> 146 us (0.980)
    dot_general x3, matrix products: 2.7 us -> 4.96 us  [expert_rows(): up_pre = jnp.dot(rows_in, up_w, preferred_element_type=jnp.float32)]
    dot_general x9, matrix products: 13.7 us -> 11.6 us  [contract_last(): lax.dot_general(left, right, (((1,), (1,)), ((), ())), preferred_element_...]
    ppermute x4 -> x5, waiting for transfers between devices: 15.3 us -> 13.6 us  [send(): lax.ppermute(value.astype(jnp.bfloat16), 'etp', perm).astype(jnp.float32)]
    unnamed x29 -> x22, local copies, waits for them, and re-layouts: 4.7 us -> 3.12 us
  transfers between devices with their start and end apart: 14 -> 15, of which waited for: 12 -> 12; matrix products, arithmetic and copies ran while one was open for 21% -> 21% of each run, Pallas kernels for 0% -> 0%
where the time goes in v2:
time: 146 us
  matrix products  39.7 us (27%)
  waiting for transfers between devices  38.6 us (26%)
  blocking collectives  31.4 us (22%)
  starting transfers between devices  23.5 us (16%)
  local copies, waits for them, and re-layouts  6.84 us (5%)
  other arithmetic  4.32 us (3%)
    all_to_all x1, blocking collectives, shards(): lax.all_to_all(send, 'expert', split_axis=0, concat_axis=0, tiled=True)  17.9 us
    ppermute x5, waiting for transfers between devices, send(): lax.ppermute(value.astype(jnp.bfloat16), 'etp', perm).astype(jnp.float32)  13.6 us
    all_to_all x1, blocking collectives, shards(): lax.all_to_all(back, 'expert', split_axis=0, concat_axis=0, tiled=True)  13.5 us
    dot_general x3, matrix products, contract_first(): lax.dot_general(left, right, (((0,), (0,)), ((), ())), preferred_element_...  12.4 us
    ppermute x1, waiting for transfers between devices, etp_gather(): first = lax.ppermute(chip, 'etp', onward)  11.6 us
    dot_general x9, matrix products, contract_last(): lax.dot_general(left, right, (((1,), (1,)), ((), ())), preferred_element_...  11.6 us
    ppermute x1, waiting for transfers between devices, etp_gather(): second = lax.ppermute(first[:, 0], 'etp', onward)  6.01 us
    dot_general x3, matrix products, expert_rows(): up_pre = jnp.dot(rows_in, up_w, preferred_element_type=jnp.float32)  4.96 us
  transfers between devices with their start and end apart: 15, of which 12 were waited for; matrix products, arithmetic and copies ran while one was open for 21% of the time, Pallas kernels for 0%

profile of v2, /device:TPU:1, one launch (start us, length us, event | category | flops | bytes accessed | tf_op | source)
XLA Modules:
  0.0 145.7 jit_solution(15229331682669298736)
XLA Ops:
  6.5 17.9 %all_to_all.10 = bf16[16,4,4096]{2,1,0:T(4,128)(2,1)S(1)} all-to-all(bf16[16,4,4096]{2,1,0:T(4,128)(2,1)S(1)} %reshape.232), channel_id=1, replica_groups=mesh['expert'=16,'etp'=8] {'expert'}, dimensions={0} | all-to-all | bytes 1048576 | tf_op jit(solution)/shard_map/all_to_all | solution.py:110
  24.5 2.1 %collective-permute-start = (bf16[64,4096]{1,0:T(8,128)(2,1)S(1)}, bf16[64,4096]{1,0:T(8,128)(2,1)S(1)}, u32[]{:S(2)}, u32[]{:S(2)}) collective-permute-start(bf16[64,4096]{1,0:T(8,128)(2,1)S(1)} %reshape.233), channel_id=1, source_target_pairs={{0,1},{1,0},{2,3},{3,2},{4,5},{5,4},{6,7},{7,6},{8,9},{9,8},{10,11... | collective-permute-start | bytes 1572872 | tf_op jit(solution)/shard_map/ppermute | solution.py:115
  28.2 3.8 %collective-permute-start.1 = (bf16[2,64,4096]{2,1,0:T(8,128)(2,1)S(1)}, bf16[2,64,4096]{2,1,0:T(8,128)(2,1)S(1)}, u32[]{:S(2)}, u32[]{:S(2)}) collective-permute-start(bf16[2,64,4096]{2,1,0:T(8,128)(2,1)S(1)} %pad_maximum_fusion.2), channel_id=1, source_target_pairs={{0,2},{1,7},{2,4},{3,1},{4,6},{5,3},{6,0},{7,5},{8,10},{9,15},{10,... | collective-permute-start | bytes 3145736 | tf_op jit(solution)/shard_map/ppermute | solution.py:116
  32.0 2.9 %fusion.22 = f32[128,896]{1,0:T(8,128)S(1)} fusion(bf16[1,2048,896]{2,1,0:T(8,128)(2,1)} %param.12, bf16[128,4096]{1,0:T(8,128)(2,1)S(1)} %bitcast.184), kind=kOutput, calls=%fused_computation.22 | convolution fusion | flops 469762048 | bytes 4653056 | tf_op jit(solution)/shard_map/dot_general | solution.py:27
  41.8 2.0 %collective-permute-done.1 = bf16[2,64,4096]{2,1,0:T(8,128)(2,1)S(1)} collective-permute-done((bf16[2,64,4096]{2,1,0:T(8,128)(2,1)S(1)}, bf16[2,64,4096]{2,1,0:T(8,128)(2,1)S(1)}, u32[]{:S(2)}, u32[]{:S(2)}) %collective-permute-start.1) | collective-permute-done | bytes 1048608 | tf_op jit(solution)/shard_map/ppermute | solution.py:116
  43.8 1.7 %collective-permute-start.3 = (bf16[2,64,4096]{2,1,0:T(8,128)(2,1)S(1)}, bf16[2,64,4096]{2,1,0:T(8,128)(2,1)S(1)}, u32[]{:S(2)}, u32[]{:S(2)}) collective-permute-start(bf16[2,64,4096]{2,1,0:T(8,128)(2,1)S(1)} %collective-permute-done.1), channel_id=1, source_target_pairs={{0,1},{1,0},{2,3},{3,2},{4,5},{5,4},{6,7},{7,6},{8,9},{9,8},{10,11... | collective-permute-start | bytes 3145736 | tf_op jit(solution)/shard_map/ppermute | solution.py:121
  45.5 2.0 %collective-permute-start.2 = (bf16[64,4096]{1,0:T(8,128)(2,1)S(1)}, bf16[64,4096]{1,0:T(8,128)(2,1)S(1)}, u32[]{:S(2)}, u32[]{:S(2)}) collective-permute-start(bf16[64,4096]{1,0:T(8,128)(2,1)S(1)} %slice_bitcast_fusion.3), channel_id=1, source_target_pairs={{0,2},{1,7},{2,4},{3,1},{4,6},{5,3},{6,0},{7,5},{8,10},{9,15},{10,... | collective-permute-start | bytes 1572872 | tf_op jit(solution)/shard_map/ppermute | solution.py:120
  50.5 1.6 %multiply_convert_fusion.1 = (bf16[256,896]{1,0:T(8,128)(2,1)S(1)}, bf16[256,896]{1,0:T(8,128)(2,1)S(1)}, bf16[256,896]{1,0:T(8,128)(2,1)S(1)}) fusion(f32[256,896]{1,0:T(8,128)S(1)} %fusion.4, f32[256,896]{1,0:T(8,128)S(1)} %fusion.18, bf16[1,2048,896]{2,1,0:T(8,128)(2,1)S(1)} %copy-done.3, bf16[256,4096]{1,0:T(8,128)(2,1)S(1)} %bitcast.190), kind=kOutput, calls=%fused_computation.91 | convolution fusion | flops 942964736 | bytes 7929856 | tf_op jit(solution)/shard_map/dot_general | solution.py:26
  66.5 3.9 %convolution_convert_fusion.2 = bf16[896,2048]{1,0:T(8,128)(2,1)} fusion(bf16[128,2048]{1,0:T(8,128)(2,1)S(1)} %get-tuple-element.52, bf16[256,2048]{1,0:T(8,128)(2,1)S(1)} %get-tuple-element.45, bf16[128,2048]{1,0:T(8,128)(2,1)S(1)} %get-tuple-element.50, bf16[128,896]{1,0:T(8,128)(2,1)S(1)} %get-tuple-element.61, ...), kind=kOutput, calls=%fused_computation.38 | convolution fusion | flops 1889927168 | bytes 6684672 | tf_op jit(solution)/shard_map/dot_general | solution.py:16
  70.8 4.9 %collective-permute-done.7 = bf16[2,64,2048]{2,1,0:T(8,128)(2,1)S(1)} collective-permute-done((bf16[2,64,2048]{2,1,0:T(8,128)(2,1)S(1)}, bf16[2,64,2048]{2,1,0:T(8,128)(2,1)S(1)}, u32[]{:S(2)}, u32[]{:S(2)}) %collective-permute-start.7) | collective-permute-done | bytes 524320 | tf_op jit(solution)/shard_map/ppermute | solution.py:67
  76.4 4.2 %convolution_convert_fusion = bf16[2048,896]{1,0:T(8,128)(2,1)} fusion(bf16[128,896]{1,0:T(8,128)(2,1)S(1)} %get-tuple-element.63, bf16[256,896]{1,0:T(8,128)(2,1)S(1)} %get-tuple-element.35, bf16[128,896]{1,0:T(8,128)(2,1)S(1)} %get-tuple-element.34, bf16[128,2048]{1,0:T(8,128)(2,1)S(1)} %get-tuple-element.51, ...), kind=kOutput, calls=%fused_computation.36 | convolution fusion | flops 1889927168 | bytes 6684672 | tf_op jit(solution)/shard_map/dot_general | solution.py:16
  80.6 4.2 %convolution_convert_fusion.1 = bf16[2048,896]{1,0:T(8,128)(2,1)} fusion(bf16[128,896]{1,0:T(8,128)(2,1)S(1)} %get-tuple-element.62, bf16[256,896]{1,0:T(8,128)(2,1)S(1)} %get-tuple-element.33, bf16[128,896]{1,0:T(8,128)(2,1)S(1)} %get-tuple-element.32, bf16[128,2048]{1,0:T(8,128)(2,1)S(1)} %get-tuple-element.51, ...), kind=kOutput, calls=%fused_computation.37 | convolution fusion | flops 1889927168 | bytes 6684672 | tf_op jit(solution)/shard_map/dot_general | solution.py:16
  84.8 6.3 %collective-permute-done.8 = bf16[2,2,64,2048]{3,2,1,0:T(8,128)(2,1)S(1)} collective-permute-done((bf16[2,2,64,2048]{3,2,1,0:T(8,128)(2,1)S(1)}, bf16[2,2,64,2048]{3,2,1,0:T(8,128)(2,1)S(1)}, u32[]{:S(2)}, u32[]{:S(2)}) %collective-permute-start.8) | collective-permute-done | bytes 1048608 | tf_op jit(solution)/shard_map/ppermute | solution.py:67
  92.8 1.5 %collective-permute-done.9 = bf16[2,64,2048]{2,1,0:T(8,128)(2,1)S(1)} collective-permute-done((bf16[2,64,2048]{2,1,0:T(8,128)(2,1)S(1)}, bf16[2,64,2048]{2,1,0:T(8,128)(2,1)S(1)}, u32[]{:S(2)}, u32[]{:S(2)}) %collective-permute-start.9) | collective-permute-done | bytes 524320 | tf_op jit(solution)/shard_map/ppermute | solution.py:67
  95.1 13.5 %all_to_all.11 = bf16[16,8,2048]{2,1,0:T(8,128)(2,1)S(1)} all-to-all(bf16[16,8,2048]{2,1,0:T(8,128)(2,1)S(1)} %pad_maximum_fusion.10), channel_id=1, replica_groups=mesh['expert'=16,'etp'=8] {'expert'}, dimensions={0} | all-to-all | bytes 1048576 | tf_op jit(solution)/shard_map/all_to_all | solution.py:165
  109.1 1.9 %collective-permute-start.10 = (bf16[2,64,2048]{2,1,0:T(8,128)(2,1)S(1)}, bf16[2,64,2048]{2,1,0:T(8,128)(2,1)S(1)}, u32[]{:S(2)}, u32[]{:S(2)}) collective-permute-start(bf16[2,64,2048]{2,1,0:T(8,128)(2,1)S(1)} %reshape.237), channel_id=1, source_target_pairs={{0,1},{1,0},{2,3},{3,2},{4,5},{5,4},{6,7},{7,6},{8,9},{9,8},{10,11... | collective-permute-start | bytes 1572872 | tf_op jit(solution)/shard_map/ppermute | solution.py:51
  111.1 1.4 collective-permute-done.10
  112.6 3.5 %collective-permute-start.11 = (bf16[2,2,64,2048]{3,2,0,1:T(8,128)(2,1)S(1)}, bf16[2,2,64,2048]{3,2,0,1:T(8,128)(2,1)S(1)}, u32[]{:S(2)}, u32[]{:S(2)}) collective-permute-start(bf16[2,2,64,2048]{3,2,0,1:T(8,128)(2,1)S(1)} %pad_maximum_fusion.5), channel_id=1, source_target_pairs={{0,2},{1,7},{2,4},{3,1},{4,6},{5,3},{6,0},{7,5},{8,10},{9,15},{10,... | collective-permute-start | bytes 3145736 | tf_op jit(solution)/shard_map/ppermute | solution.py:52
  116.3 11.6 %collective-permute-done.11 = bf16[2,2,64,2048]{3,2,0,1:T(8,128)(2,1)S(1)} collective-permute-done((bf16[2,2,64,2048]{3,2,0,1:T(8,128)(2,1)S(1)}, bf16[2,2,64,2048]{3,2,0,1:T(8,128)(2,1)S(1)}, u32[]{:S(2)}, u32[]{:S(2)}) %collective-permute-start.11) | collective-permute-done | bytes 1048608 | tf_op jit(solution)/shard_map/ppermute | solution.py:52
  127.9 3.2 %collective-permute-start.12 = (bf16[2,64,2048]{2,1,0:T(8,128)(2,1)S(1)}, bf16[2,64,2048]{2,1,0:T(8,128)(2,1)S(1)}, u32[]{:S(2)}, u32[]{:S(2)}) collective-permute-start(bf16[2,64,2048]{2,1,0:T(8,128)(2,1)S(1)} %slice_bitcast_fusion.2), channel_id=1, source_target_pairs={{0,2},{1,7},{2,4},{3,1},{4,6},{5,3},{6,0},{7,5},{8,10},{9,15},{10,... | collective-permute-start | bytes 1572872 | tf_op jit(solution)/shard_map/ppermute | solution.py:55
  131.2 6.0 %collective-permute-done.12 = bf16[2,64,2048]{2,1,0:T(8,128)(2,1)S(1)} collective-permute-done((bf16[2,64,2048]{2,1,0:T(8,128)(2,1)S(1)}, bf16[2,64,2048]{2,1,0:T(8,128)(2,1)S(1)}, u32[]{:S(2)}, u32[]{:S(2)}) %collective-permute-start.12) | collective-permute-done | bytes 524320 | tf_op jit(solution)/shard_map/ppermute | solution.py:55
  137.2 2.8 %collective-permute-start.14 = (bf16[2,64,2048]{2,1,0:T(8,128)(2,1)S(1)}, bf16[2,64,2048]{2,1,0:T(8,128)(2,1)S(1)}, u32[]{:S(2)}, u32[]{:S(2)}) collective-permute-start(bf16[2,64,2048]{2,1,0:T(8,128)(2,1)S(1)} %collective-permute-done.12), channel_id=1, source_target_pairs={{0,1},{1,0},{2,3},{3,2},{4,5},{5,4},{6,7},{7,6},{8,9},{9,8},{10,11... | collective-permute-start | bytes 1572872 | tf_op jit(solution)/shard_map/ppermute | solution.py:57
  142.2 1.6 %convolution_reduce_fusion = bf16[128,2048]{1,0:T(8,128)(2,1)} fusion(bf16[512,2048,1]{1,0,2:T(8,128)(2,1)S(1)} %bitcast.195, s32[128,2]{0,1:T(2,128)S(1)} %get-tuple-element.77), kind=kOutput, calls=%fused_computation.57 | convolution fusion | flops 537264128 | bytes 2622464 | tf_op jit(solution)/shard_map/dot_general | solution.py:22
  143.9 1.8 %multiply_reduce_fusion = (f32[128,2]{0,1:T(2,128)}, bf16[128,2048]{1,0:T(8,128)(2,1)}) fusion(f32[128,2048]{1,0:T(8,128)S(1)} %convert_element_type.148, f32[128,2]{0,1:T(2,128)S(1)} %copy-done.6, bf16[512,2048,1]{1,0,2:T(8,128)(2,1)S(1)} %bitcast.194, s32[128,2]{0,1:T(2,128)S(1)} %get-tuple-element.77), kind=kOutput, calls=%fused_computation.54 | convolution fusion | flops 538836736 | bytes 3673088 | tf_op jit(solution)/shard_map/dot_general | solution.py:22
  (113 shorter events, 38.0 us)
Async XLA Ops:
  0.6 4.1 %copy-start = (bf16[128,2048]{1,0:T(8,128)(2,1)S(1)}, bf16[128,2048]{1,0:T(8,128)(2,1)}, u32[]{:S(2)}) copy-start(bf16[128,2048]{1,0:T(8,128)(2,1)} %param.7) | copy-start | bytes 1572868
  24.5 3.6 %collective-permute-start = (bf16[64,4096]{1,0:T(8,128)(2,1)S(1)}, bf16[64,4096]{1,0:T(8,128)(2,1)S(1)}, u32[]{:S(2)}, u32[]{:S(2)}) collective-permute-start(bf16[64,4096]{1,0:T(8,128)(2,1)S(1)} %reshape.233), channel_id=1, source_target_pairs={{0,1},{1,0},{2,3},{3,2},{4,5},{5,4},{6,7},{7,6},{8,9},{9,8},{10,11... | collective-permute-start | bytes 1572872 | tf_op jit(solution)/shard_map/ppermute | solution.py:115
  26.7 8.3 %copy-start.4 = (bf16[1,896,2048]{2,1,0:T(8,128)(2,1)S(1)}, bf16[1,896,2048]{2,1,0:T(8,128)(2,1)}, u32[]{:S(2)}) copy-start(bf16[1,896,2048]{2,1,0:T(8,128)(2,1)} %param.13) | copy-start | bytes 11010052
  28.2 15.6 %collective-permute-start.1 = (bf16[2,64,4096]{2,1,0:T(8,128)(2,1)S(1)}, bf16[2,64,4096]{2,1,0:T(8,128)(2,1)S(1)}, u32[]{:S(2)}, u32[]{:S(2)}) collective-permute-start(bf16[2,64,4096]{2,1,0:T(8,128)(2,1)S(1)} %pad_maximum_fusion.2), channel_id=1, source_target_pairs={{0,2},{1,7},{2,4},{3,1},{4,6},{5,3},{6,0},{7,5},{8,10},{9,15},{10,... | collective-permute-start | bytes 3145736 | tf_op jit(solution)/shard_map/ppermute | solution.py:116
  32.0 4.2 %copy-start.3 = (bf16[1,2048,896]{2,1,0:T(8,128)(2,1)S(1)}, bf16[1,2048,896]{2,1,0:T(8,128)(2,1)}, u32[]{:S(2)}) copy-start(bf16[1,2048,896]{2,1,0:T(8,128)(2,1)} %param.11) | copy-start | bytes 11010052
  36.3 2.0 %copy-start.2 = (bf16[1,2048,896]{2,1,0:T(8,128)(2,1)S(1)}, bf16[1,2048,896]{2,1,0:T(8,128)(2,1)}, u32[]{:S(2)}) copy-start(bf16[1,2048,896]{2,1,0:T(8,128)(2,1)} %param.12) | copy-start | bytes 11010052
  43.8 4.0 %collective-permute-start.3 = (bf16[2,64,4096]{2,1,0:T(8,128)(2,1)S(1)}, bf16[2,64,4096]{2,1,0:T(8,128)(2,1)S(1)}, u32[]{:S(2)}, u32[]{:S(2)}) collective-permute-start(bf16[2,64,4096]{2,1,0:T(8,128)(2,1)S(1)} %collective-permute-done.1), channel_id=1, source_target_pairs={{0,1},{1,0},{2,3},{3,2},{4,5},{5,4},{6,7},{7,6},{8,9},{9,8},{10,11... | collective-permute-start | bytes 3145736 | tf_op jit(solution)/shard_map/ppermute | solution.py:121
  45.5 10.4 %collective-permute-start.2 = (bf16[64,4096]{1,0:T(8,128)(2,1)S(1)}, bf16[64,4096]{1,0:T(8,128)(2,1)S(1)}, u32[]{:S(2)}, u32[]{:S(2)}) collective-permute-start(bf16[64,4096]{1,0:T(8,128)(2,1)S(1)} %slice_bitcast_fusion.3), channel_id=1, source_target_pairs={{0,2},{1,7},{2,4},{3,1},{4,6},{5,3},{6,0},{7,5},{8,10},{9,15},{10,... | collective-permute-start | bytes 1572872 | tf_op jit(solution)/shard_map/ppermute | solution.py:120
  56.0 2.0 %collective-permute-start.5 = (bf16[64,4096]{1,0:T(8,128)(2,1)S(1)}, bf16[64,4096]{1,0:T(8,128)(2,1)S(1)}, u32[]{:S(2)}, u32[]{:S(2)}) collective-permute-start(bf16[64,4096]{1,0:T(8,128)(2,1)S(1)} %collective-permute-done.2), channel_id=1, source_target_pairs={{0,1},{1,0},{2,3},{3,2},{4,5},{5,4},{6,7},{7,6},{8,9},{9,8},{10,11... | collective-permute-start | bytes 1572872 | tf_op jit(solution)/shard_map/ppermute | solution.py:125
  64.3 2.0 %collective-permute-start.6 = (bf16[2,64,2048]{2,1,0:T(8,128)(2,1)S(1)}, bf16[2,64,2048]{2,1,0:T(8,128)(2,1)S(1)}, u32[]{:S(2)}, u32[]{:S(2)}) collective-permute-start(bf16[2,64,2048]{2,1,0:T(8,128)(2,1)S(1)} %pad_maximum_fusion.9), channel_id=1, source_target_pairs={{0,1},{1,0},{2,3},{3,2},{4,5},{5,4},{6,7},{7,6},{8,9},{9,8},{10,11... | collective-permute-start | bytes 1572872 | tf_op jit(solution)/shard_map/ppermute | solution.py:67
  64.9 5.6 %collective-permute-start.4 = (bf16[2,2,64,2048]{3,2,1,0:T(8,128)(2,1)S(1)}, bf16[2,2,64,2048]{3,2,1,0:T(8,128)(2,1)S(1)}, u32[]{:S(2)}, u32[]{:S(2)}) collective-permute-start(bf16[2,2,64,2048]{3,2,1,0:T(8,128)(2,1)S(1)} %pad_maximum_fusion.3), channel_id=1, source_target_pairs={{0,1},{1,0},{2,3},{3,2},{4,5},{5,4},{6,7},{7,6},{8,9},{9,8},{10,11... | collective-permute-start | bytes 3145736 | tf_op jit(solution)/shard_map/ppermute | solution.py:67
  66.4 9.3 %collective-permute-start.7 = (bf16[2,64,2048]{2,1,0:T(8,128)(2,1)S(1)}, bf16[2,64,2048]{2,1,0:T(8,128)(2,1)S(1)}, u32[]{:S(2)}, u32[]{:S(2)}) collective-permute-start(bf16[2,64,2048]{2,1,0:T(8,128)(2,1)S(1)} %add_convert_fusion), channel_id=1, source_target_pairs={{2,0},{7,1},{4,2},{1,3},{6,4},{3,5},{0,6},{5,7},{10,8},{15,9},{12,... | collective-permute-start | bytes 1572872 | tf_op jit(solution)/shard_map/ppermute | solution.py:67
  76.2 14.9 %collective-permute-start.8 = (bf16[2,2,64,2048]{3,2,1,0:T(8,128)(2,1)S(1)}, bf16[2,2,64,2048]{3,2,1,0:T(8,128)(2,1)S(1)}, u32[]{:S(2)}, u32[]{:S(2)}) collective-permute-start(bf16[2,2,64,2048]{3,2,1,0:T(8,128)(2,1)S(1)} %pad_maximum_fusion.4), channel_id=1, source_target_pairs={{2,0},{7,1},{4,2},{1,3},{6,4},{3,5},{0,6},{5,7},{10,8},{15,9},{12,... | collective-permute-start | bytes 3145736 | tf_op jit(solution)/shard_map/ppermute | solution.py:67
  91.8 2.6 %collective-permute-start.9 = (bf16[2,64,2048]{2,1,0:T(8,128)(2,1)S(1)}, bf16[2,64,2048]{2,1,0:T(8,128)(2,1)S(1)}, u32[]{:S(2)}, u32[]{:S(2)}) collective-permute-start(bf16[2,64,2048]{2,1,0:T(8,128)(2,1)S(1)} %fusion.80), channel_id=1, source_target_pairs={{0,1},{1,0},{2,3},{3,2},{4,5},{5,4},{6,7},{7,6},{8,9},{9,8},{10,11... | collective-permute-start | bytes 1572872 | tf_op jit(solution)/shard_map/ppermute | solution.py:67
  95.1 21.1 %copy-start.5 = (bf16[128,2048]{1,0:T(8,128)(2,1)S(1)}, bf16[128,2048]{1,0:T(8,128)(2,1)}, u32[]{:S(2)}) copy-start(bf16[128,2048]{1,0:T(8,128)(2,1)} %param.8) | copy-start | bytes 1572868
  109.1 3.4 %collective-permute-start.10 = (bf16[2,64,2048]{2,1,0:T(8,128)(2,1)S(1)}, bf16[2,64,2048]{2,1,0:T(8,128)(2,1)S(1)}, u32[]{:S(2)}, u32[]{:S(2)}) collective-permute-start(bf16[2,64,2048]{2,1,0:T(8,128)(2,1)S(1)} %reshape.237), channel_id=1, source_target_pairs={{0,1},{1,0},{2,3},{3,2},{4,5},{5,4},{6,7},{7,6},{8,9},{9,8},{10,11... | collective-permute-start | bytes 1572872 | tf_op jit(solution)/shard_map/ppermute | solution.py:51
  112.6 15.2 %collective-permute-start.11 = (bf16[2,2,64,2048]{3,2,0,1:T(8,128)(2,1)S(1)}, bf16[2,2,64,2048]{3,2,0,1:T(8,128)(2,1)S(1)}, u32[]{:S(2)}, u32[]{:S(2)}) collective-permute-start(bf16[2,2,64,2048]{3,2,0,1:T(8,128)(2,1)S(1)} %pad_maximum_fusion.5), channel_id=1, source_target_pairs={{0,2},{1,7},{2,4},{3,1},{4,6},{5,3},{6,0},{7,5},{8,10},{9,15},{10,... | collective-permute-start | bytes 3145736 | tf_op jit(solution)/shard_map/ppermute | solution.py:52
  127.9 9.3 %collective-permute-start.12 = (bf16[2,64,2048]{2,1,0:T(8,128)(2,1)S(1)}, bf16[2,64,2048]{2,1,0:T(8,128)(2,1)S(1)}, u32[]{:S(2)}, u32[]{:S(2)}) collective-permute-start(bf16[2,64,2048]{2,1,0:T(8,128)(2,1)S(1)} %slice_bitcast_fusion.2), channel_id=1, source_target_pairs={{0,2},{1,7},{2,4},{3,1},{4,6},{5,3},{6,0},{7,5},{8,10},{9,15},{10,... | collective-permute-start | bytes 1572872 | tf_op jit(solution)/shard_map/ppermute | solution.py:55
  131.1 9.0 %collective-permute-start.13 = (bf16[2,2,64,2048]{3,2,0,1:T(8,128)(2,1)S(1)}, bf16[2,2,64,2048]{3,2,0,1:T(8,128)(2,1)S(1)}, u32[]{:S(2)}, u32[]{:S(2)}) collective-permute-start(bf16[2,2,64,2048]{3,2,0,1:T(8,128)(2,1)S(1)} %collective-permute-done.11), channel_id=1, source_target_pairs={{0,1},{1,0},{2,3},{3,2},{4,5},{5,4},{6,7},{7,6},{8,9},{9,8},{10,11... | collective-permute-start | bytes 3145736 | tf_op jit(solution)/shard_map/ppermute | solution.py:56
  137.2 4.4 %collective-permute-start.14 = (bf16[2,64,2048]{2,1,0:T(8,128)(2,1)S(1)}, bf16[2,64,2048]{2,1,0:T(8,128)(2,1)S(1)}, u32[]{:S(2)}, u32[]{:S(2)}) collective-permute-start(bf16[2,64,2048]{2,1,0:T(8,128)(2,1)S(1)} %collective-permute-done.12), channel_id=1, source_target_pairs={{0,1},{1,0},{2,3},{3,2},{4,5},{5,4},{6,7},{7,6},{8,9},{9,8},{10,11... | collective-permute-start | bytes 1572872 | tf_op jit(solution)/shard_map/ppermute | solution.py:57
  141.6 2.2 %copy-start.6 = (f32[128,2]{0,1:T(2,128)S(1)}, f32[128,2]{0,1:T(2,128)}, u32[]{:S(2)}) copy-start(f32[128,2]{0,1:T(2,128)} %param.10) | copy-start | bytes 3076
  142.2 3.4 %copy-start.1 = (bf16[128,2048]{1,0:T(8,128)(2,1)S(1)}, bf16[128,2048]{1,0:T(8,128)(2,1)}, u32[]{:S(2)}) copy-start(bf16[128,2048]{1,0:T(8,128)(2,1)} %param.7) | copy-start | bytes 1572868

commit v3 on v2

--- a/solution.py
+++ b/solution.py
@@ -60,13 +60,14 @@
     ), cover
 
 
-def etp_reduce(part, split_count, cover_near=None, cover_far=None):
+def etp_reduce(part, split_count, cover_near=None, cover_far=None, pair=None):
     swap, _, backward = etp_perms(split_count)
 
     def send(value, perm):
         return lax.ppermute(value.astype(jnp.bfloat16), "etp", perm).astype(jnp.float32)
 
-    pair = send(jnp.stack([part[5], part[6]], axis=0), swap)
+    if pair is None:
+        pair = send(jnp.stack([part[5], part[6]], axis=0), swap)
     arrived = send(part[4] + send(part[7], swap), backward)
     arrived, cover_near = lax.optimization_barrier((arrived, cover_near))
     near = part[2] + pair[0] + arrived
@@ -122,9 +123,22 @@
     pieces.append(jnp.concatenate([first, first_other], axis=0).reshape(4 * place_count, 2 * features))
     results.append(expert_rows(pieces[1][:, :features], pieces[1][:, features:], *weights))
     second, results[1] = lax.optimization_barrier((second, results[1]))
+    partner_rows = slice(2 * place_count, 4 * place_count)
+    pair = lax.ppermute(
+        jnp.stack(
+            [
+                part_rows.astype(jnp.bfloat16)[partner_rows].reshape(2, place_count, features)
+                for part_rows in results[1][:2]
+            ],
+            axis=1,
+        ),
+        "etp",
+        swap,
+    ).astype(jnp.float32)
     second_other = lax.ppermute(second, "etp", swap)
     pieces.append(jnp.concatenate([second, second_other], axis=0))
     results.append(expert_rows(pieces[2][:, :features], pieces[2][:, features:], *weights))
+    pair, results[2] = lax.optimization_barrier((pair, results[2]))
 
     rows_in = jnp.concatenate([piece[:, :features] for piece in pieces], axis=0)
     rows_grad = jnp.concatenate([piece[:, features:] for piece in pieces], axis=0)
@@ -153,6 +167,7 @@
             contract_first(rows_in, gate_grad).astype(jnp.bfloat16),
             contract_first(rows_in, up_grad).astype(jnp.bfloat16),
         ),
+        pair,
     )
     sums = sums.astype(jnp.bfloat16)
     back = jnp.concatenate(

time: 146 us -> 147 us (level)
    ppermute x5 -> x4, waiting for transfers between devices: 13.6 us -> 14.3 us  [send(): lax.ppermute(value.astype(jnp.bfloat16), 'etp', perm).astype(jnp.float32)]
  transfers between devices with their start and end apart: 15 -> 15, of which waited for: 12 -> 12; matrix products, arithmetic and copies ran while one was open for 21% -> 25% of each run, Pallas kernels for 0% -> 0%
where the time goes in v3:
time: 147 us; the launch traced here: 146 us
  matrix products  39.8 us (27%)
  waiting for transfers between devices  39.2 us (27%)
  blocking collectives  31.4 us (21%)
  starting transfers between devices  23.5 us (16%)
  local copies, waits for them, and re-layouts  6.81 us (5%)
  other arithmetic  4.21 us (3%)
    all_to_all x1, blocking collectives, shards(): lax.all_to_all(send, 'expert', split_axis=0, concat_axis=0, tiled=True)  17.9 us
    ppermute x4, waiting for transfers between devices, send(): lax.ppermute(value.astype(jnp.bfloat16), 'etp', perm).astype(jnp.float32)  14.3 us
    all_to_all x1, blocking collectives, shards(): lax.all_to_all(back, 'expert', split_axis=0, concat_axis=0, tiled=True)  13.5 us
    dot_general x3, matrix products, contract_first(): lax.dot_general(left, right, (((0,), (0,)), ((), ())), preferred_element_...  12.4 us
    ppermute x1, waiting for transfers between devices, etp_gather(): first = lax.ppermute(chip, 'etp', onward)  11.6 us
    dot_general x9, matrix products, contract_last(): lax.dot_general(left, right, (((1,), (1,)), ((), ())), preferred_element_...  11.6 us
    ppermute x1, waiting for transfers between devices, etp_gather(): second = lax.ppermute(first[:, 0], 'etp', onward)  6.01 us
    dot_general x4, matrix products, select_rows(): jnp.dot(selector.astype(table.dtype), table, preferred_element_type=jnp.f...  4.91 us
  transfers between devices with their start and end apart: 15, of which 12 were waited for; matrix products, arithmetic and copies ran while one was open for 25% of the time, Pallas kernels for 0%

profile of v3, /device:TPU:1, one launch (start us, length us, event | category | flops | bytes accessed | tf_op | source)
XLA Modules:
  0.0 146.2 jit_solution(10039030306645721405)
XLA Ops:
  6.5 17.9 %all_to_all.10 = bf16[16,4,4096]{2,1,0:T(4,128)(2,1)S(1)} all-to-all(bf16[16,4,4096]{2,1,0:T(4,128)(2,1)S(1)} %reshape.232), channel_id=1, replica_groups=mesh['expert'=16,'etp'=8] {'expert'}, dimensions={0} | all-to-all | bytes 1048576 | tf_op jit(solution)/shard_map/all_to_all | solution.py:111
  24.5 2.1 %collective-permute-start = (bf16[64,4096]{1,0:T(8,128)(2,1)S(1)}, bf16[64,4096]{1,0:T(8,128)(2,1)S(1)}, u32[]{:S(2)}, u32[]{:S(2)}) collective-permute-start(bf16[64,4096]{1,0:T(8,128)(2,1)S(1)} %reshape.233), channel_id=1, source_target_pairs={{0,1},{1,0},{2,3},{3,2},{4,5},{5,4},{6,7},{7,6},{8,9},{9,8},{10,11... | collective-permute-start | bytes 1572872 | tf_op jit(solution)/shard_map/ppermute | solution.py:116
  28.2 3.8 %collective-permute-start.1 = (bf16[2,64,4096]{2,1,0:T(8,128)(2,1)S(1)}, bf16[2,64,4096]{2,1,0:T(8,128)(2,1)S(1)}, u32[]{:S(2)}, u32[]{:S(2)}) collective-permute-start(bf16[2,64,4096]{2,1,0:T(8,128)(2,1)S(1)} %pad_maximum_fusion.2), channel_id=1, source_target_pairs={{0,2},{1,7},{2,4},{3,1},{4,6},{5,3},{6,0},{7,5},{8,10},{9,15},{10,... | collective-permute-start | bytes 3145736 | tf_op jit(solution)/shard_map/ppermute | solution.py:117
  32.0 2.9 %fusion.22 = f32[128,896]{1,0:T(8,128)S(1)} fusion(bf16[1,2048,896]{2,1,0:T(8,128)(2,1)} %param.12, bf16[128,4096]{1,0:T(8,128)(2,1)S(1)} %bitcast.172), kind=kOutput, calls=%fused_computation.22 | convolution fusion | flops 469762048 | bytes 4653056 | tf_op jit(solution)/shard_map/dot_general | solution.py:27
  41.8 2.0 %collective-permute-done.1 = bf16[2,64,4096]{2,1,0:T(8,128)(2,1)S(1)} collective-permute-done((bf16[2,64,4096]{2,1,0:T(8,128)(2,1)S(1)}, bf16[2,64,4096]{2,1,0:T(8,128)(2,1)S(1)}, u32[]{:S(2)}, u32[]{:S(2)}) %collective-permute-start.1) | collective-permute-done | bytes 1048608 | tf_op jit(solution)/shard_map/ppermute | solution.py:117
  43.8 1.7 %collective-permute-start.3 = (bf16[2,64,4096]{2,1,0:T(8,128)(2,1)S(1)}, bf16[2,64,4096]{2,1,0:T(8,128)(2,1)S(1)}, u32[]{:S(2)}, u32[]{:S(2)}) collective-permute-start(bf16[2,64,4096]{2,1,0:T(8,128)(2,1)S(1)} %collective-permute-done.1), channel_id=1, source_target_pairs={{0,1},{1,0},{2,3},{3,2},{4,5},{5,4},{6,7},{7,6},{8,9},{9,8},{10,11... | collective-permute-start | bytes 3145736 | tf_op jit(solution)/shard_map/ppermute | solution.py:122
  45.5 2.0 %collective-permute-start.2 = (bf16[64,4096]{1,0:T(8,128)(2,1)S(1)}, bf16[64,4096]{1,0:T(8,128)(2,1)S(1)}, u32[]{:S(2)}, u32[]{:S(2)}) collective-permute-start(bf16[64,4096]{1,0:T(8,128)(2,1)S(1)} %slice_bitcast_fusion.2), channel_id=1, source_target_pairs={{0,2},{1,7},{2,4},{3,1},{4,6},{5,3},{6,0},{7,5},{8,10},{9,15},{10,... | collective-permute-start | bytes 1572872 | tf_op jit(solution)/shard_map/ppermute | solution.py:121
  50.5 1.6 %multiply_convert_fusion.1 = (bf16[256,896]{1,0:T(8,128)(2,1)S(1)}, bf16[256,896]{1,0:T(8,128)(2,1)S(1)}, bf16[256,896]{1,0:T(8,128)(2,1)S(1)}) fusion(f32[256,896]{1,0:T(8,128)S(1)} %fusion.4, f32[256,896]{1,0:T(8,128)S(1)} %fusion.18, bf16[1,2048,896]{2,1,0:T(8,128)(2,1)S(1)} %copy-done.4, bf16[256,4096]{1,0:T(8,128)(2,1)S(1)} %bitcast.178), kind=kOutput, calls=%fused_computation.87 | convolution fusion | flops 942964736 | bytes 7929856 | tf_op jit(solution)/shard_map/dot_general | solution.py:26
  67.0 3.9 %convolution_convert_fusion.2 = bf16[896,2048]{1,0:T(8,128)(2,1)} fusion(bf16[128,2048]{1,0:T(8,128)(2,1)S(1)} %get-tuple-element.64, bf16[256,2048]{1,0:T(8,128)(2,1)S(1)} %get-tuple-element.57, bf16[128,2048]{1,0:T(8,128)(2,1)S(1)} %get-tuple-element.62, bf16[128,896]{1,0:T(8,128)(2,1)S(1)} %get-tuple-element.40, ...), kind=kOutput, calls=%fused_computation.38 | convolution fusion | flops 1889927168 | bytes 6684672 | tf_op jit(solution)/shard_map/dot_general | solution.py:16
  71.1 5.2 %collective-permute-done.7 = bf16[2,64,2048]{2,1,0:T(8,128)(2,1)S(1)} collective-permute-done((bf16[2,64,2048]{2,1,0:T(8,128)(2,1)S(1)}, bf16[2,64,2048]{2,1,0:T(8,128)(2,1)S(1)}, u32[]{:S(2)}, u32[]{:S(2)}) %collective-permute-start.7) | collective-permute-done | bytes 524320 | tf_op jit(solution)/shard_map/ppermute | solution.py:67
  76.9 4.2 %convolution_convert_fusion = bf16[2048,896]{1,0:T(8,128)(2,1)} fusion(bf16[128,896]{1,0:T(8,128)(2,1)S(1)} %get-tuple-element.47, bf16[256,896]{1,0:T(8,128)(2,1)S(1)} %get-tuple-element.46, bf16[128,896]{1,0:T(8,128)(2,1)S(1)} %get-tuple-element.45, bf16[128,2048]{1,0:T(8,128)(2,1)S(1)} %get-tuple-element.63, ...), kind=kOutput, calls=%fused_computation.36 | convolution fusion | flops 1889927168 | bytes 6684672 | tf_op jit(solution)/shard_map/dot_general | solution.py:16
  81.1 4.2 %convolution_convert_fusion.1 = bf16[2048,896]{1,0:T(8,128)(2,1)} fusion(bf16[128,896]{1,0:T(8,128)(2,1)S(1)} %get-tuple-element.44, bf16[256,896]{1,0:T(8,128)(2,1)S(1)} %get-tuple-element.43, bf16[128,896]{1,0:T(8,128)(2,1)S(1)} %get-tuple-element.42, bf16[128,2048]{1,0:T(8,128)(2,1)S(1)} %get-tuple-element.63, ...), kind=kOutput, calls=%fused_computation.37 | convolution fusion | flops 1889927168 | bytes 6684672 | tf_op jit(solution)/shard_map/dot_general | solution.py:16
  85.3 6.3 %collective-permute-done.8 = bf16[2,2,64,2048]{3,2,1,0:T(8,128)(2,1)S(1)} collective-permute-done((bf16[2,2,64,2048]{3,2,1,0:T(8,128)(2,1)S(1)}, bf16[2,2,64,2048]{3,2,1,0:T(8,128)(2,1)S(1)}, u32[]{:S(2)}, u32[]{:S(2)}) %collective-permute-start.8) | collective-permute-done | bytes 1048608 | tf_op jit(solution)/shard_map/ppermute | solution.py:67
  93.4 1.5 %collective-permute-done.9 = bf16[2,64,2048]{2,1,0:T(8,128)(2,1)S(1)} collective-permute-done((bf16[2,64,2048]{2,1,0:T(8,128)(2,1)S(1)}, bf16[2,64,2048]{2,1,0:T(8,128)(2,1)S(1)}, u32[]{:S(2)}, u32[]{:S(2)}) %collective-permute-start.9) | collective-permute-done | bytes 524320 | tf_op jit(solution)/shard_map/ppermute | solution.py:67
  95.6 13.5 %all_to_all.11 = bf16[16,8,2048]{2,1,0:T(8,128)(2,1)S(1)} all-to-all(bf16[16,8,2048]{2,1,0:T(8,128)(2,1)S(1)} %pad_maximum_fusion.10), channel_id=1, replica_groups=mesh['expert'=16,'etp'=8] {'expert'}, dimensions={0} | all-to-all | bytes 1048576 | tf_op jit(solution)/shard_map/all_to_all | solution.py:180
  109.7 1.9 %collective-permute-start.10 = (bf16[2,64,2048]{2,1,0:T(8,128)(2,1)S(1)}, bf16[2,64,2048]{2,1,0:T(8,128)(2,1)S(1)}, u32[]{:S(2)}, u32[]{:S(2)}) collective-permute-start(bf16[2,64,2048]{2,1,0:T(8,128)(2,1)S(1)} %reshape.237), channel_id=1, source_target_pairs={{0,1},{1,0},{2,3},{3,2},{4,5},{5,4},{6,7},{7,6},{8,9},{9,8},{10,11... | collective-permute-start | bytes 1572872 | tf_op jit(solution)/shard_map/ppermute | solution.py:51
  111.6 1.4 collective-permute-done.10
  113.2 3.5 %collective-permute-start.11 = (bf16[2,2,64,2048]{3,2,0,1:T(8,128)(2,1)S(1)}, bf16[2,2,64,2048]{3,2,0,1:T(8,128)(2,1)S(1)}, u32[]{:S(2)}, u32[]{:S(2)}) collective-permute-start(bf16[2,2,64,2048]{3,2,0,1:T(8,128)(2,1)S(1)} %pad_maximum_fusion.5), channel_id=1, source_target_pairs={{0,2},{1,7},{2,4},{3,1},{4,6},{5,3},{6,0},{7,5},{8,10},{9,15},{10,... | collective-permute-start | bytes 3145736 | tf_op jit(solution)/shard_map/ppermute | solution.py:52
  116.8 11.6 %collective-permute-done.11 = bf16[2,2,64,2048]{3,2,0,1:T(8,128)(2,1)S(1)} collective-permute-done((bf16[2,2,64,2048]{3,2,0,1:T(8,128)(2,1)S(1)}, bf16[2,2,64,2048]{3,2,0,1:T(8,128)(2,1)S(1)}, u32[]{:S(2)}, u32[]{:S(2)}) %collective-permute-start.11) | collective-permute-done | bytes 1048608 | tf_op jit(solution)/shard_map/ppermute | solution.py:52
  128.4 3.2 %collective-permute-start.12 = (bf16[2,64,2048]{2,1,0:T(8,128)(2,1)S(1)}, bf16[2,64,2048]{2,1,0:T(8,128)(2,1)S(1)}, u32[]{:S(2)}, u32[]{:S(2)}) collective-permute-start(bf16[2,64,2048]{2,1,0:T(8,128)(2,1)S(1)} %slice_bitcast_fusion.1), channel_id=1, source_target_pairs={{0,2},{1,7},{2,4},{3,1},{4,6},{5,3},{6,0},{7,5},{8,10},{9,15},{10,... | collective-permute-start | bytes 1572872 | tf_op jit(solution)/shard_map/ppermute | solution.py:55
  131.7 6.0 %collective-permute-done.12 = bf16[2,64,2048]{2,1,0:T(8,128)(2,1)S(1)} collective-permute-done((bf16[2,64,2048]{2,1,0:T(8,128)(2,1)S(1)}, bf16[2,64,2048]{2,1,0:T(8,128)(2,1)S(1)}, u32[]{:S(2)}, u32[]{:S(2)}) %collective-permute-start.12) | collective-permute-done | bytes 524320 | tf_op jit(solution)/shard_map/ppermute | solution.py:55
  137.7 2.8 %collective-permute-start.14 = (bf16[2,64,2048]{2,1,0:T(8,128)(2,1)S(1)}, bf16[2,64,2048]{2,1,0:T(8,128)(2,1)S(1)}, u32[]{:S(2)}, u32[]{:S(2)}) collective-permute-start(bf16[2,64,2048]{2,1,0:T(8,128)(2,1)S(1)} %collective-permute-done.12), channel_id=1, source_target_pairs={{0,1},{1,0},{2,3},{3,2},{4,5},{5,4},{6,7},{7,6},{8,9},{9,8},{10,11... | collective-permute-start | bytes 1572872 | tf_op jit(solution)/shard_map/ppermute | solution.py:57
  142.8 1.6 %convolution_reduce_fusion = bf16[128,2048]{1,0:T(8,128)(2,1)} fusion(bf16[512,2048,1]{1,0,2:T(8,128)(2,1)S(1)} %bitcast.185, s32[128,2]{0,1:T(2,128)S(1)} %get-tuple-element.85), kind=kOutput, calls=%fused_computation.55 | convolution fusion | flops 537264128 | bytes 2622464 | tf_op jit(solution)/shard_map/dot_general | solution.py:22
  144.4 1.8 %multiply_reduce_fusion = (f32[128,2]{0,1:T(2,128)}, bf16[128,2048]{1,0:T(8,128)(2,1)}) fusion(f32[128,2048]{1,0:T(8,128)S(1)} %convert_element_type.141, f32[128,2]{0,1:T(2,128)S(1)} %copy-done.6, bf16[512,2048,1]{1,0,2:T(8,128)(2,1)S(1)} %bitcast.184, s32[128,2]{0,1:T(2,128)S(1)} %get-tuple-element.85), kind=kOutput, calls=%fused_computation.52 | convolution fusion | flops 538836736 | bytes 3673088 | tf_op jit(solution)/shard_map/dot_general | solution.py:22
  (113 shorter events, 38.2 us)
Async XLA Ops:
  0.6 4.1 %copy-start = (bf16[128,2048]{1,0:T(8,128)(2,1)S(1)}, bf16[128,2048]{1,0:T(8,128)(2,1)}, u32[]{:S(2)}) copy-start(bf16[128,2048]{1,0:T(8,128)(2,1)} %param.7) | copy-start | bytes 1572868
  24.5 3.6 %collective-permute-start = (bf16[64,4096]{1,0:T(8,128)(2,1)S(1)}, bf16[64,4096]{1,0:T(8,128)(2,1)S(1)}, u32[]{:S(2)}, u32[]{:S(2)}) collective-permute-start(bf16[64,4096]{1,0:T(8,128)(2,1)S(1)} %reshape.233), channel_id=1, source_target_pairs={{0,1},{1,0},{2,3},{3,2},{4,5},{5,4},{6,7},{7,6},{8,9},{9,8},{10,11... | collective-permute-start | bytes 1572872 | tf_op jit(solution)/shard_map/ppermute | solution.py:116
  26.7 8.3 %copy-start.3 = (bf16[1,896,2048]{2,1,0:T(8,128)(2,1)S(1)}, bf16[1,896,2048]{2,1,0:T(8,128)(2,1)}, u32[]{:S(2)}) copy-start(bf16[1,896,2048]{2,1,0:T(8,128)(2,1)} %param.13) | copy-start | bytes 11010052
  28.2 15.6 %collective-permute-start.1 = (bf16[2,64,4096]{2,1,0:T(8,128)(2,1)S(1)}, bf16[2,64,4096]{2,1,0:T(8,128)(2,1)S(1)}, u32[]{:S(2)}, u32[]{:S(2)}) collective-permute-start(bf16[2,64,4096]{2,1,0:T(8,128)(2,1)S(1)} %pad_maximum_fusion.2), channel_id=1, source_target_pairs={{0,2},{1,7},{2,4},{3,1},{4,6},{5,3},{6,0},{7,5},{8,10},{9,15},{10,... | collective-permute-start | bytes 3145736 | tf_op jit(solution)/shard_map/ppermute | solution.py:117
  32.0 4.2 %copy-start.4 = (bf16[1,2048,896]{2,1,0:T(8,128)(2,1)S(1)}, bf16[1,2048,896]{2,1,0:T(8,128)(2,1)}, u32[]{:S(2)}) copy-start(bf16[1,2048,896]{2,1,0:T(8,128)(2,1)} %param.11) | copy-start | bytes 11010052
  36.3 2.0 %copy-start.2 = (bf16[1,2048,896]{2,1,0:T(8,128)(2,1)S(1)}, bf16[1,2048,896]{2,1,0:T(8,128)(2,1)}, u32[]{:S(2)}) copy-start(bf16[1,2048,896]{2,1,0:T(8,128)(2,1)} %param.12) | copy-start | bytes 11010052
  43.8 4.0 %collective-permute-start.3 = (bf16[2,64,4096]{2,1,0:T(8,128)(2,1)S(1)}, bf16[2,64,4096]{2,1,0:T(8,128)(2,1)S(1)}, u32[]{:S(2)}, u32[]{:S(2)}) collective-permute-start(bf16[2,64,4096]{2,1,0:T(8,128)(2,1)S(1)} %collective-permute-done.1), channel_id=1, source_target_pairs={{0,1},{1,0},{2,3},{3,2},{4,5},{5,4},{6,7},{7,6},{8,9},{9,8},{10,11... | collective-permute-start | bytes 3145736 | tf_op jit(solution)/shard_map/ppermute | solution.py:122
  45.5 10.4 %collective-permute-start.2 = (bf16[64,4096]{1,0:T(8,128)(2,1)S(1)}, bf16[64,4096]{1,0:T(8,128)(2,1)S(1)}, u32[]{:S(2)}, u32[]{:S(2)}) collective-permute-start(bf16[64,4096]{1,0:T(8,128)(2,1)S(1)} %slice_bitcast_fusion.2), channel_id=1, source_target_pairs={{0,2},{1,7},{2,4},{3,1},{4,6},{5,3},{6,0},{7,5},{8,10},{9,15},{10,... | collective-permute-start | bytes 1572872 | tf_op jit(solution)/shard_map/ppermute | solution.py:121
  56.0 2.0 %collective-permute-start.5 = (bf16[64,4096]{1,0:T(8,128)(2,1)S(1)}, bf16[64,4096]{1,0:T(8,128)(2,1)S(1)}, u32[]{:S(2)}, u32[]{:S(2)}) collective-permute-start(bf16[64,4096]{1,0:T(8,128)(2,1)S(1)} %collective-permute-done.2), channel_id=1, source_target_pairs={{0,1},{1,0},{2,3},{3,2},{4,5},{5,4},{6,7},{7,6},{8,9},{9,8},{10,11... | collective-permute-start | bytes 1572872 | tf_op jit(solution)/shard_map/ppermute | solution.py:138
  56.6 7.6 %collective-permute-start.4 = (bf16[2,2,64,2048]{3,2,1,0:T(8,128)(2,1)S(1)}, bf16[2,2,64,2048]{3,2,1,0:T(8,128)(2,1)S(1)}, u32[]{:S(2)}, u32[]{:S(2)}) collective-permute-start(bf16[2,2,64,2048]{3,2,1,0:T(8,128)(2,1)S(1)} %pad_maximum_fusion.3), channel_id=1, source_target_pairs={{0,1},{1,0},{2,3},{3,2},{4,5},{5,4},{6,7},{7,6},{8,9},{9,8},{10,11... | collective-permute-start | bytes 3145736 | tf_op jit(solution)/shard_map/ppermute | solution.py:127
  64.6 2.2 %collective-permute-start.6 = (bf16[2,64,2048]{2,1,0:T(8,128)(2,1)S(1)}, bf16[2,64,2048]{2,1,0:T(8,128)(2,1)S(1)}, u32[]{:S(2)}, u32[]{:S(2)}) collective-permute-start(bf16[2,64,2048]{2,1,0:T(8,128)(2,1)S(1)} %pad_maximum_fusion.9), channel_id=1, source_target_pairs={{0,1},{1,0},{2,3},{3,2},{4,5},{5,4},{6,7},{7,6},{8,9},{9,8},{10,11... | collective-permute-start | bytes 1572872 | tf_op jit(solution)/shard_map/ppermute | solution.py:67
  67.0 9.3 %collective-permute-start.7 = (bf16[2,64,2048]{2,1,0:T(8,128)(2,1)S(1)}, bf16[2,64,2048]{2,1,0:T(8,128)(2,1)S(1)}, u32[]{:S(2)}, u32[]{:S(2)}) collective-permute-start(bf16[2,64,2048]{2,1,0:T(8,128)(2,1)S(1)} %add_convert_fusion.1), channel_id=1, source_target_pairs={{2,0},{7,1},{4,2},{1,3},{6,4},{3,5},{0,6},{5,7},{10,8},{15,9},{12,... | collective-permute-start | bytes 1572872 | tf_op jit(solution)/shard_map/ppermute | solution.py:67
  76.7 14.9 %collective-permute-start.8 = (bf16[2,2,64,2048]{3,2,1,0:T(8,128)(2,1)S(1)}, bf16[2,2,64,2048]{3,2,1,0:T(8,128)(2,1)S(1)}, u32[]{:S(2)}, u32[]{:S(2)}) collective-permute-start(bf16[2,2,64,2048]{3,2,1,0:T(8,128)(2,1)S(1)} %pad_maximum_fusion.4), channel_id=1, source_target_pairs={{2,0},{7,1},{4,2},{1,3},{6,4},{3,5},{0,6},{5,7},{10,8},{15,9},{12,... | collective-permute-start | bytes 3145736 | tf_op jit(solution)/shard_map/ppermute | solution.py:67
  92.3 2.6 %collective-permute-start.9 = (bf16[2,64,2048]{2,1,0:T(8,128)(2,1)S(1)}, bf16[2,64,2048]{2,1,0:T(8,128)(2,1)S(1)}, u32[]{:S(2)}, u32[]{:S(2)}) collective-permute-start(bf16[2,64,2048]{2,1,0:T(8,128)(2,1)S(1)} %fusion.72), channel_id=1, source_target_pairs={{0,1},{1,0},{2,3},{3,2},{4,5},{5,4},{6,7},{7,6},{8,9},{9,8},{10,11... | collective-permute-start | bytes 1572872 | tf_op jit(solution)/shard_map/ppermute | solution.py:67
  95.6 21.1 %copy-start.5 = (bf16[128,2048]{1,0:T(8,128)(2,1)S(1)}, bf16[128,2048]{1,0:T(8,128)(2,1)}, u32[]{:S(2)}) copy-start(bf16[128,2048]{1,0:T(8,128)(2,1)} %param.8) | copy-start | bytes 1572868
  109.7 3.4 %collective-permute-start.10 = (bf16[2,64,2048]{2,1,0:T(8,128)(2,1)S(1)}, bf16[2,64,2048]{2,1,0:T(8,128)(2,1)S(1)}, u32[]{:S(2)}, u32[]{:S(2)}) collective-permute-start(bf16[2,64,2048]{2,1,0:T(8,128)(2,1)S(1)} %reshape.237), channel_id=1, source_target_pairs={{0,1},{1,0},{2,3},{3,2},{4,5},{5,4},{6,7},{7,6},{8,9},{9,8},{10,11... | collective-permute-start | bytes 1572872 | tf_op jit(solution)/shard_map/ppermute | solution.py:51
  113.2 15.2 %collective-permute-start.11 = (bf16[2,2,64,2048]{3,2,0,1:T(8,128)(2,1)S(1)}, bf16[2,2,64,2048]{3,2,0,1:T(8,128)(2,1)S(1)}, u32[]{:S(2)}, u32[]{:S(2)}) collective-permute-start(bf16[2,2,64,2048]{3,2,0,1:T(8,128)(2,1)S(1)} %pad_maximum_fusion.5), channel_id=1, source_target_pairs={{0,2},{1,7},{2,4},{3,1},{4,6},{5,3},{6,0},{7,5},{8,10},{9,15},{10,... | collective-permute-start | bytes 3145736 | tf_op jit(solution)/shard_map/ppermute | solution.py:52
  128.4 9.3 %collective-permute-start.12 = (bf16[2,64,2048]{2,1,0:T(8,128)(2,1)S(1)}, bf16[2,64,2048]{2,1,0:T(8,128)(2,1)S(1)}, u32[]{:S(2)}, u32[]{:S(2)}) collective-permute-start(bf16[2,64,2048]{2,1,0:T(8,128)(2,1)S(1)} %slice_bitcast_fusion.1), channel_id=1, source_target_pairs={{0,2},{1,7},{2,4},{3,1},{4,6},{5,3},{6,0},{7,5},{8,10},{9,15},{10,... | collective-permute-start | bytes 1572872 | tf_op jit(solution)/shard_map/ppermute | solution.py:55
  131.6 9.0 %collective-permute-start.13 = (bf16[2,2,64,2048]{3,2,0,1:T(8,128)(2,1)S(1)}, bf16[2,2,64,2048]{3,2,0,1:T(8,128)(2,1)S(1)}, u32[]{:S(2)}, u32[]{:S(2)}) collective-permute-start(bf16[2,2,64,2048]{3,2,0,1:T(8,128)(2,1)S(1)} %collective-permute-done.11), channel_id=1, source_target_pairs={{0,1},{1,0},{2,3},{3,2},{4,5},{5,4},{6,7},{7,6},{8,9},{9,8},{10,11... | collective-permute-start | bytes 3145736 | tf_op jit(solution)/shard_map/ppermute | solution.py:56
  137.7 4.4 %collective-permute-start.14 = (bf16[2,64,2048]{2,1,0:T(8,128)(2,1)S(1)}, bf16[2,64,2048]{2,1,0:T(8,128)(2,1)S(1)}, u32[]{:S(2)}, u32[]{:S(2)}) collective-permute-start(bf16[2,64,2048]{2,1,0:T(8,128)(2,1)S(1)} %collective-permute-done.12), channel_id=1, source_target_pairs={{0,1},{1,0},{2,3},{3,2},{4,5},{5,4},{6,7},{7,6},{8,9},{9,8},{10,11... | collective-permute-start | bytes 1572872 | tf_op jit(solution)/shard_map/ppermute | solution.py:57
  142.2 2.2 %copy-start.6 = (f32[128,2]{0,1:T(2,128)S(1)}, f32[128,2]{0,1:T(2,128)}, u32[]{:S(2)}) copy-start(f32[128,2]{0,1:T(2,128)} %param.10) | copy-start | bytes 3076
  142.8 3.4 %copy-start.1 = (bf16[128,2048]{1,0:T(8,128)(2,1)S(1)}, bf16[128,2048]{1,0:T(8,128)(2,1)}, u32[]{:S(2)}) copy-start(bf16[128,2048]{1,0:T(8,128)(2,1)} %param.7) | copy-start | bytes 1572868

commit v4 on v2

--- a/solution.py
+++ b/solution.py
@@ -101,12 +101,11 @@
     pick = local_place[None, :] == jnp.arange(place_count, dtype=jnp.int32)[:, None]
     pick_tokens = jnp.any(pick.reshape(place_count, token_count, TOP), axis=2)
 
-    send_rows = select_rows(pick_tokens, tokens).astype(jnp.bfloat16)
     place_weight = jnp.sum(jnp.where(pick, combine_weights.reshape(1, pair_count), 0.0), axis=1)
-    send_grad = (place_weight[:, None] * select_rows(pick_tokens, out_grad)).astype(jnp.bfloat16)
-    send = jnp.concatenate([send_rows, send_grad], axis=1).reshape(
-        expert_count, per_split, 2 * features
-    )
+    picked = select_rows(pick_tokens, jnp.concatenate([tokens, out_grad], axis=1))
+    send = jnp.concatenate(
+        [picked[:, :features], place_weight[:, None] * picked[:, features:]], axis=1
+    ).astype(jnp.bfloat16).reshape(expert_count, per_split, 2 * features)
     recv = lax.all_to_all(send, "expert", split_axis=0, concat_axis=0, tiled=True)
     unit = recv.reshape(place_count, 2 * features)
 
@@ -184,11 +183,11 @@
     table_row = (slot_of * expert_count + flat_routes) * per_split + slots % per_split
     gather = table_row[:, None] == jnp.arange(row_total, dtype=jnp.int32)[None, :]
     out_pairs = select_rows(gather, out_table).reshape(token_count, TOP, features)
-    input_pairs = select_rows(gather, input_table).reshape(token_count, TOP, features)
     grad_values = out_grad.astype(jnp.float32)
     mixed = jnp.sum(combine_weights[:, :, None] * out_pairs, axis=1).astype(jnp.bfloat16)
     combine_grad = jnp.sum(grad_values[:, None, :] * out_pairs, axis=2)
-    tokens_grad = jnp.sum(input_pairs, axis=1).astype(jnp.bfloat16)
+    token_gather = jnp.any(gather.reshape(token_count, TOP, row_total), axis=1)
+    tokens_grad = select_rows(token_gather, input_table).astype(jnp.bfloat16)
     return (
         mixed,
         tokens_grad,

time: 146 us -> 146 us (level)
    dot_general x4 -> x3, matrix products: 4.91 us -> 4.55 us  [select_rows(): jnp.dot(selector.astype(table.dtype), table, preferred_element_type=jnp.f...]
    unnamed x22 -> x18, local copies, waits for them, and re-layouts: 3.12 us -> 3.04 us
where the time goes in v4:
time: 146 us
  matrix products  39.3 us (27%)
  waiting for transfers between devices  38.5 us (26%)
  blocking collectives  31.4 us (22%)
  starting transfers between devices  23.5 us (16%)
  local copies, waits for them, and re-layouts  6.88 us (5%)
  other arithmetic  4.83 us (3%)
    all_to_all x1, blocking collectives, shards(): lax.all_to_all(send, 'expert', split_axis=0, concat_axis=0, tiled=True)  17.9 us
    ppermute x5, waiting for transfers between devices, send(): lax.ppermute(value.astype(jnp.bfloat16), 'etp', perm).astype(jnp.float32)  13.7 us
    all_to_all x1, blocking collectives, shards(): lax.all_to_all(back, 'expert', split_axis=0, concat_axis=0, tiled=True)  13.5 us
    dot_general x3, matrix products, contract_first(): lax.dot_general(left, right, (((0,), (0,)), ((), ())), preferred_element_...  12.4 us
    dot_general x9, matrix products, contract_last(): lax.dot_general(left, right, (((1,), (1,)), ((), ())), preferred_element_...  11.6 us
    ppermute x1, waiting for transfers between devices, etp_gather(): first = lax.ppermute(chip, 'etp', onward)  11.5 us
    ppermute x1, waiting for transfers between devices, etp_gather(): second = lax.ppermute(first[:, 0], 'etp', onward)  6.01 us
    dot_general x3, matrix products, expert_rows(): up_pre = jnp.dot(rows_in, up_w, preferred_element_type=jnp.float32)  4.96 us
  transfers between devices with their start and end apart: 15, of which 12 were waited for; matrix products, arithmetic and copies ran while one was open for 21% of the time, Pallas kernels for 0%

profile of v4, /device:TPU:1, one launch (start us, length us, event | category | flops | bytes accessed | tf_op | source)
XLA Modules:
  0.0 145.7 jit_solution(8572159191662355537)
XLA Ops:
  4.6 1.5 %fusion.62 = f32[64,4096]{1,0:T(8,128)S(1)} fusion(pred[64,128]{1,0:T(8,128)(4,1)S(1)} %fusion.92, bf16[128,2048]{1,0:T(8,128)(2,1)} %param.8, bf16[128,2048]{1,0:T(8,128)(2,1)} %param.7), kind=kOutput, calls=%fused_computation.65 | convolution fusion | flops 69206016 | bytes 2105344 | tf_op jit(solution)/shard_map/dot_general | solution.py:22
  6.9 17.9 %all_to_all.10 = bf16[16,4,4096]{2,1,0:T(4,128)(2,1)S(1)} all-to-all(bf16[16,4,4096]{2,1,0:T(4,128)(2,1)S(1)} %pad_maximum_fusion.8), channel_id=1, replica_groups=mesh['expert'=16,'etp'=8] {'expert'}, dimensions={0} | all-to-all | bytes 1048576 | tf_op jit(solution)/shard_map/all_to_all | solution.py:109
  24.9 2.1 %collective-permute-start = (bf16[64,4096]{1,0:T(8,128)(2,1)S(1)}, bf16[64,4096]{1,0:T(8,128)(2,1)S(1)}, u32[]{:S(2)}, u32[]{:S(2)}) collective-permute-start(bf16[64,4096]{1,0:T(8,128)(2,1)S(1)} %reshape.228), channel_id=1, source_target_pairs={{0,1},{1,0},{2,3},{3,2},{4,5},{5,4},{6,7},{7,6},{8,9},{9,8},{10,11... | collective-permute-start | bytes 1572872 | tf_op jit(solution)/shard_map/ppermute | solution.py:114
  28.6 3.8 %collective-permute-start.1 = (bf16[2,64,4096]{2,1,0:T(8,128)(2,1)S(1)}, bf16[2,64,4096]{2,1,0:T(8,128)(2,1)S(1)}, u32[]{:S(2)}, u32[]{:S(2)}) collective-permute-start(bf16[2,64,4096]{2,1,0:T(8,128)(2,1)S(1)} %pad_maximum_fusion.2), channel_id=1, source_target_pairs={{0,2},{1,7},{2,4},{3,1},{4,6},{5,3},{6,0},{7,5},{8,10},{9,15},{10,... | collective-permute-start | bytes 3145736 | tf_op jit(solution)/shard_map/ppermute | solution.py:115
  32.4 2.9 %fusion.22 = f32[128,896]{1,0:T(8,128)S(1)} fusion(bf16[1,2048,896]{2,1,0:T(8,128)(2,1)} %param.12, bf16[128,4096]{1,0:T(8,128)(2,1)S(1)} %bitcast.179), kind=kOutput, calls=%fused_computation.22 | convolution fusion | flops 469762048 | bytes 4653056 | tf_op jit(solution)/shard_map/dot_general | solution.py:27
  42.1 2.0 %collective-permute-done.1 = bf16[2,64,4096]{2,1,0:T(8,128)(2,1)S(1)} collective-permute-done((bf16[2,64,4096]{2,1,0:T(8,128)(2,1)S(1)}, bf16[2,64,4096]{2,1,0:T(8,128)(2,1)S(1)}, u32[]{:S(2)}, u32[]{:S(2)}) %collective-permute-start.1) | collective-permute-done | bytes 1048608 | tf_op jit(solution)/shard_map/ppermute | solution.py:115
  44.2 1.7 %collective-permute-start.3 = (bf16[2,64,4096]{2,1,0:T(8,128)(2,1)S(1)}, bf16[2,64,4096]{2,1,0:T(8,128)(2,1)S(1)}, u32[]{:S(2)}, u32[]{:S(2)}) collective-permute-start(bf16[2,64,4096]{2,1,0:T(8,128)(2,1)S(1)} %collective-permute-done.1), channel_id=1, source_target_pairs={{0,1},{1,0},{2,3},{3,2},{4,5},{5,4},{6,7},{7,6},{8,9},{9,8},{10,11... | collective-permute-start | bytes 3145736 | tf_op jit(solution)/shard_map/ppermute | solution.py:120
  45.9 2.0 %collective-permute-start.2 = (bf16[64,4096]{1,0:T(8,128)(2,1)S(1)}, bf16[64,4096]{1,0:T(8,128)(2,1)S(1)}, u32[]{:S(2)}, u32[]{:S(2)}) collective-permute-start(bf16[64,4096]{1,0:T(8,128)(2,1)S(1)} %slice_bitcast_fusion.3), channel_id=1, source_target_pairs={{0,2},{1,7},{2,4},{3,1},{4,6},{5,3},{6,0},{7,5},{8,10},{9,15},{10,... | collective-permute-start | bytes 1572872 | tf_op jit(solution)/shard_map/ppermute | solution.py:119
  50.9 1.6 %multiply_convert_fusion.1 = (bf16[256,896]{1,0:T(8,128)(2,1)S(1)}, bf16[256,896]{1,0:T(8,128)(2,1)S(1)}, bf16[256,896]{1,0:T(8,128)(2,1)S(1)}) fusion(f32[256,896]{1,0:T(8,128)S(1)} %fusion.4, f32[256,896]{1,0:T(8,128)S(1)} %fusion.18, bf16[1,2048,896]{2,1,0:T(8,128)(2,1)S(1)} %copy-done.1, bf16[256,4096]{1,0:T(8,128)(2,1)S(1)} %bitcast.185), kind=kOutput, calls=%fused_computation.92 | convolution fusion | flops 942964736 | bytes 7929856 | tf_op jit(solution)/shard_map/dot_general | solution.py:26
  66.9 3.9 %convolution_convert_fusion.2 = bf16[896,2048]{1,0:T(8,128)(2,1)} fusion(bf16[128,2048]{1,0:T(8,128)(2,1)S(1)} %get-tuple-element.52, bf16[256,2048]{1,0:T(8,128)(2,1)S(1)} %get-tuple-element.45, bf16[128,2048]{1,0:T(8,128)(2,1)S(1)} %get-tuple-element.50, bf16[128,896]{1,0:T(8,128)(2,1)S(1)} %get-tuple-element.61, ...), kind=kOutput, calls=%fused_computation.38 | convolution fusion | flops 1889927168 | bytes 6684672 | tf_op jit(solution)/shard_map/dot_general | solution.py:16
  71.2 4.9 %collective-permute-done.7 = bf16[2,64,2048]{2,1,0:T(8,128)(2,1)S(1)} collective-permute-done((bf16[2,64,2048]{2,1,0:T(8,128)(2,1)S(1)}, bf16[2,64,2048]{2,1,0:T(8,128)(2,1)S(1)}, u32[]{:S(2)}, u32[]{:S(2)}) %collective-permute-start.7) | collective-permute-done | bytes 524320 | tf_op jit(solution)/shard_map/ppermute | solution.py:67
  76.8 4.2 %convolution_convert_fusion = bf16[2048,896]{1,0:T(8,128)(2,1)} fusion(bf16[128,896]{1,0:T(8,128)(2,1)S(1)} %get-tuple-element.63, bf16[256,896]{1,0:T(8,128)(2,1)S(1)} %get-tuple-element.35, bf16[128,896]{1,0:T(8,128)(2,1)S(1)} %get-tuple-element.34, bf16[128,2048]{1,0:T(8,128)(2,1)S(1)} %get-tuple-element.51, ...), kind=kOutput, calls=%fused_computation.36 | convolution fusion | flops 1889927168 | bytes 6684672 | tf_op jit(solution)/shard_map/dot_general | solution.py:16
  81.0 4.2 %convolution_convert_fusion.1 = bf16[2048,896]{1,0:T(8,128)(2,1)} fusion(bf16[128,896]{1,0:T(8,128)(2,1)S(1)} %get-tuple-element.62, bf16[256,896]{1,0:T(8,128)(2,1)S(1)} %get-tuple-element.33, bf16[128,896]{1,0:T(8,128)(2,1)S(1)} %get-tuple-element.32, bf16[128,2048]{1,0:T(8,128)(2,1)S(1)} %get-tuple-element.51, ...), kind=kOutput, calls=%fused_computation.37 | convolution fusion | flops 1889927168 | bytes 6684672 | tf_op jit(solution)/shard_map/dot_general | solution.py:16
  85.2 6.3 %collective-permute-done.8 = bf16[2,2,64,2048]{3,2,1,0:T(8,128)(2,1)S(1)} collective-permute-done((bf16[2,2,64,2048]{3,2,1,0:T(8,128)(2,1)S(1)}, bf16[2,2,64,2048]{3,2,1,0:T(8,128)(2,1)S(1)}, u32[]{:S(2)}, u32[]{:S(2)}) %collective-permute-start.8) | collective-permute-done | bytes 1048608 | tf_op jit(solution)/shard_map/ppermute | solution.py:67
  93.2 1.5 %collective-permute-done.9 = bf16[2,64,2048]{2,1,0:T(8,128)(2,1)S(1)} collective-permute-done((bf16[2,64,2048]{2,1,0:T(8,128)(2,1)S(1)}, bf16[2,64,2048]{2,1,0:T(8,128)(2,1)S(1)}, u32[]{:S(2)}, u32[]{:S(2)}) %collective-permute-start.9) | collective-permute-done | bytes 524320 | tf_op jit(solution)/shard_map/ppermute | solution.py:67
  95.5 13.5 %all_to_all.11 = bf16[16,8,2048]{2,1,0:T(8,128)(2,1)S(1)} all-to-all(bf16[16,8,2048]{2,1,0:T(8,128)(2,1)S(1)} %pad_maximum_fusion.10), channel_id=1, replica_groups=mesh['expert'=16,'etp'=8] {'expert'}, dimensions={0} | all-to-all | bytes 1048576 | tf_op jit(solution)/shard_map/all_to_all | solution.py:164
  109.5 1.9 %collective-permute-start.10 = (bf16[2,64,2048]{2,1,0:T(8,128)(2,1)S(1)}, bf16[2,64,2048]{2,1,0:T(8,128)(2,1)S(1)}, u32[]{:S(2)}, u32[]{:S(2)}) collective-permute-start(bf16[2,64,2048]{2,1,0:T(8,128)(2,1)S(1)} %reshape.232), channel_id=1, source_target_pairs={{0,1},{1,0},{2,3},{3,2},{4,5},{5,4},{6,7},{7,6},{8,9},{9,8},{10,11... | collective-permute-start | bytes 1572872 | tf_op jit(solution)/shard_map/ppermute | solution.py:51
  111.5 1.4 collective-permute-done.10
  113.0 3.5 %collective-permute-start.11 = (bf16[2,2,64,2048]{3,2,0,1:T(8,128)(2,1)S(1)}, bf16[2,2,64,2048]{3,2,0,1:T(8,128)(2,1)S(1)}, u32[]{:S(2)}, u32[]{:S(2)}) collective-permute-start(bf16[2,2,64,2048]{3,2,0,1:T(8,128)(2,1)S(1)} %pad_maximum_fusion.5), channel_id=1, source_target_pairs={{0,2},{1,7},{2,4},{3,1},{4,6},{5,3},{6,0},{7,5},{8,10},{9,15},{10,... | collective-permute-start | bytes 3145736 | tf_op jit(solution)/shard_map/ppermute | solution.py:52
  116.8 11.5 %collective-permute-done.11 = bf16[2,2,64,2048]{3,2,0,1:T(8,128)(2,1)S(1)} collective-permute-done((bf16[2,2,64,2048]{3,2,0,1:T(8,128)(2,1)S(1)}, bf16[2,2,64,2048]{3,2,0,1:T(8,128)(2,1)S(1)}, u32[]{:S(2)}, u32[]{:S(2)}) %collective-permute-start.11) | collective-permute-done | bytes 1048608 | tf_op jit(solution)/shard_map/ppermute | solution.py:52
  128.3 3.2 %collective-permute-start.12 = (bf16[2,64,2048]{2,1,0:T(8,128)(2,1)S(1)}, bf16[2,64,2048]{2,1,0:T(8,128)(2,1)S(1)}, u32[]{:S(2)}, u32[]{:S(2)}) collective-permute-start(bf16[2,64,2048]{2,1,0:T(8,128)(2,1)S(1)} %slice_bitcast_fusion.2), channel_id=1, source_target_pairs={{0,2},{1,7},{2,4},{3,1},{4,6},{5,3},{6,0},{7,5},{8,10},{9,15},{10,... | collective-permute-start | bytes 1572872 | tf_op jit(solution)/shard_map/ppermute | solution.py:55
  131.6 6.0 %collective-permute-done.12 = bf16[2,64,2048]{2,1,0:T(8,128)(2,1)S(1)} collective-permute-done((bf16[2,64,2048]{2,1,0:T(8,128)(2,1)S(1)}, bf16[2,64,2048]{2,1,0:T(8,128)(2,1)S(1)}, u32[]{:S(2)}, u32[]{:S(2)}) %collective-permute-start.12) | collective-permute-done | bytes 524320 | tf_op jit(solution)/shard_map/ppermute | solution.py:55
  137.6 2.8 %collective-permute-start.14 = (bf16[2,64,2048]{2,1,0:T(8,128)(2,1)S(1)}, bf16[2,64,2048]{2,1,0:T(8,128)(2,1)S(1)}, u32[]{:S(2)}, u32[]{:S(2)}) collective-permute-start(bf16[2,64,2048]{2,1,0:T(8,128)(2,1)S(1)} %collective-permute-done.12), channel_id=1, source_target_pairs={{0,1},{1,0},{2,3},{3,2},{4,5},{5,4},{6,7},{7,6},{8,9},{9,8},{10,11... | collective-permute-start | bytes 1572872 | tf_op jit(solution)/shard_map/ppermute | solution.py:57
  143.9 1.8 %multiply_reduce_fusion = (f32[128,2]{0,1:T(2,128)}, bf16[128,2048]{1,0:T(8,128)(2,1)}) fusion(f32[128,2048]{1,0:T(8,128)S(1)} %convert_element_type.141, f32[128,2]{0,1:T(2,128)S(1)} %copy-done.4, bf16[512,2048,1]{1,0,2:T(8,128)(2,1)S(1)} %bitcast.190, s32[128,2]{0,1:T(2,128)S(1)} %get-tuple-element.77), kind=kOutput, calls=%fused_computation.52 | convolution fusion | flops 538836736 | bytes 3673088 | tf_op jit(solution)/shard_map/dot_general | solution.py:22
  (112 shorter events, 38.2 us)
Async XLA Ops:
  24.9 3.6 %collective-permute-start = (bf16[64,4096]{1,0:T(8,128)(2,1)S(1)}, bf16[64,4096]{1,0:T(8,128)(2,1)S(1)}, u32[]{:S(2)}, u32[]{:S(2)}) collective-permute-start(bf16[64,4096]{1,0:T(8,128)(2,1)S(1)} %reshape.228), channel_id=1, source_target_pairs={{0,1},{1,0},{2,3},{3,2},{4,5},{5,4},{6,7},{7,6},{8,9},{9,8},{10,11... | collective-permute-start | bytes 1572872 | tf_op jit(solution)/shard_map/ppermute | solution.py:114
  27.1 8.3 %copy-start.2 = (bf16[1,896,2048]{2,1,0:T(8,128)(2,1)S(1)}, bf16[1,896,2048]{2,1,0:T(8,128)(2,1)}, u32[]{:S(2)}) copy-start(bf16[1,896,2048]{2,1,0:T(8,128)(2,1)} %param.13) | copy-start | bytes 11010052
  28.6 15.6 %collective-permute-start.1 = (bf16[2,64,4096]{2,1,0:T(8,128)(2,1)S(1)}, bf16[2,64,4096]{2,1,0:T(8,128)(2,1)S(1)}, u32[]{:S(2)}, u32[]{:S(2)}) collective-permute-start(bf16[2,64,4096]{2,1,0:T(8,128)(2,1)S(1)} %pad_maximum_fusion.2), channel_id=1, source_target_pairs={{0,2},{1,7},{2,4},{3,1},{4,6},{5,3},{6,0},{7,5},{8,10},{9,15},{10,... | collective-permute-start | bytes 3145736 | tf_op jit(solution)/shard_map/ppermute | solution.py:115
  32.4 4.2 %copy-start.1 = (bf16[1,2048,896]{2,1,0:T(8,128)(2,1)S(1)}, bf16[1,2048,896]{2,1,0:T(8,128)(2,1)}, u32[]{:S(2)}) copy-start(bf16[1,2048,896]{2,1,0:T(8,128)(2,1)} %param.11) | copy-start | bytes 11010052
  36.7 2.0 %copy-start = (bf16[1,2048,896]{2,1,0:T(8,128)(2,1)S(1)}, bf16[1,2048,896]{2,1,0:T(8,128)(2,1)}, u32[]{:S(2)}) copy-start(bf16[1,2048,896]{2,1,0:T(8,128)(2,1)} %param.12) | copy-start | bytes 11010052
  44.2 4.0 %collective-permute-start.3 = (bf16[2,64,4096]{2,1,0:T(8,128)(2,1)S(1)}, bf16[2,64,4096]{2,1,0:T(8,128)(2,1)S(1)}, u32[]{:S(2)}, u32[]{:S(2)}) collective-permute-start(bf16[2,64,4096]{2,1,0:T(8,128)(2,1)S(1)} %collective-permute-done.1), channel_id=1, source_target_pairs={{0,1},{1,0},{2,3},{3,2},{4,5},{5,4},{6,7},{7,6},{8,9},{9,8},{10,11... | collective-permute-start | bytes 3145736 | tf_op jit(solution)/shard_map/ppermute | solution.py:120
  45.9 10.4 %collective-permute-start.2 = (bf16[64,4096]{1,0:T(8,128)(2,1)S(1)}, bf16[64,4096]{1,0:T(8,128)(2,1)S(1)}, u32[]{:S(2)}, u32[]{:S(2)}) collective-permute-start(bf16[64,4096]{1,0:T(8,128)(2,1)S(1)} %slice_bitcast_fusion.3), channel_id=1, source_target_pairs={{0,2},{1,7},{2,4},{3,1},{4,6},{5,3},{6,0},{7,5},{8,10},{9,15},{10,... | collective-permute-start | bytes 1572872 | tf_op jit(solution)/shard_map/ppermute | solution.py:119
  56.3 2.0 %collective-permute-start.5 = (bf16[64,4096]{1,0:T(8,128)(2,1)S(1)}, bf16[64,4096]{1,0:T(8,128)(2,1)S(1)}, u32[]{:S(2)}, u32[]{:S(2)}) collective-permute-start(bf16[64,4096]{1,0:T(8,128)(2,1)S(1)} %collective-permute-done.2), channel_id=1, source_target_pairs={{0,1},{1,0},{2,3},{3,2},{4,5},{5,4},{6,7},{7,6},{8,9},{9,8},{10,11... | collective-permute-start | bytes 1572872 | tf_op jit(solution)/shard_map/ppermute | solution.py:124
  64.7 2.0 %collective-permute-start.6 = (bf16[2,64,2048]{2,1,0:T(8,128)(2,1)S(1)}, bf16[2,64,2048]{2,1,0:T(8,128)(2,1)S(1)}, u32[]{:S(2)}, u32[]{:S(2)}) collective-permute-start(bf16[2,64,2048]{2,1,0:T(8,128)(2,1)S(1)} %pad_maximum_fusion.9), channel_id=1, source_target_pairs={{0,1},{1,0},{2,3},{3,2},{4,5},{5,4},{6,7},{7,6},{8,9},{9,8},{10,11... | collective-permute-start | bytes 1572872 | tf_op jit(solution)/shard_map/ppermute | solution.py:67
  65.2 5.6 %collective-permute-start.4 = (bf16[2,2,64,2048]{3,2,1,0:T(8,128)(2,1)S(1)}, bf16[2,2,64,2048]{3,2,1,0:T(8,128)(2,1)S(1)}, u32[]{:S(2)}, u32[]{:S(2)}) collective-permute-start(bf16[2,2,64,2048]{3,2,1,0:T(8,128)(2,1)S(1)} %pad_maximum_fusion.3), channel_id=1, source_target_pairs={{0,1},{1,0},{2,3},{3,2},{4,5},{5,4},{6,7},{7,6},{8,9},{9,8},{10,11... | collective-permute-start | bytes 3145736 | tf_op jit(solution)/shard_map/ppermute | solution.py:67
  66.8 9.3 %collective-permute-start.7 = (bf16[2,64,2048]{2,1,0:T(8,128)(2,1)S(1)}, bf16[2,64,2048]{2,1,0:T(8,128)(2,1)S(1)}, u32[]{:S(2)}, u32[]{:S(2)}) collective-permute-start(bf16[2,64,2048]{2,1,0:T(8,128)(2,1)S(1)} %add_convert_fusion), channel_id=1, source_target_pairs={{2,0},{7,1},{4,2},{1,3},{6,4},{3,5},{0,6},{5,7},{10,8},{15,9},{12,... | collective-permute-start | bytes 1572872 | tf_op jit(solution)/shard_map/ppermute | solution.py:67
  76.6 14.9 %collective-permute-start.8 = (bf16[2,2,64,2048]{3,2,1,0:T(8,128)(2,1)S(1)}, bf16[2,2,64,2048]{3,2,1,0:T(8,128)(2,1)S(1)}, u32[]{:S(2)}, u32[]{:S(2)}) collective-permute-start(bf16[2,2,64,2048]{3,2,1,0:T(8,128)(2,1)S(1)} %pad_maximum_fusion.4), channel_id=1, source_target_pairs={{2,0},{7,1},{4,2},{1,3},{6,4},{3,5},{0,6},{5,7},{10,8},{15,9},{12,... | collective-permute-start | bytes 3145736 | tf_op jit(solution)/shard_map/ppermute | solution.py:67
  92.2 2.6 %collective-permute-start.9 = (bf16[2,64,2048]{2,1,0:T(8,128)(2,1)S(1)}, bf16[2,64,2048]{2,1,0:T(8,128)(2,1)S(1)}, u32[]{:S(2)}, u32[]{:S(2)}) collective-permute-start(bf16[2,64,2048]{2,1,0:T(8,128)(2,1)S(1)} %fusion.83), channel_id=1, source_target_pairs={{0,1},{1,0},{2,3},{3,2},{4,5},{5,4},{6,7},{7,6},{8,9},{9,8},{10,11... | collective-permute-start | bytes 1572872 | tf_op jit(solution)/shard_map/ppermute | solution.py:67
  95.4 21.1 %copy-start.3 = (bf16[128,2048]{1,0:T(8,128)(2,1)S(1)}, bf16[128,2048]{1,0:T(8,128)(2,1)}, u32[]{:S(2)}) copy-start(bf16[128,2048]{1,0:T(8,128)(2,1)} %param.8) | copy-start | bytes 1572868
  109.5 3.4 %collective-permute-start.10 = (bf16[2,64,2048]{2,1,0:T(8,128)(2,1)S(1)}, bf16[2,64,2048]{2,1,0:T(8,128)(2,1)S(1)}, u32[]{:S(2)}, u32[]{:S(2)}) collective-permute-start(bf16[2,64,2048]{2,1,0:T(8,128)(2,1)S(1)} %reshape.232), channel_id=1, source_target_pairs={{0,1},{1,0},{2,3},{3,2},{4,5},{5,4},{6,7},{7,6},{8,9},{9,8},{10,11... | collective-permute-start | bytes 1572872 | tf_op jit(solution)/shard_map/ppermute | solution.py:51
  113.0 15.2 %collective-permute-start.11 = (bf16[2,2,64,2048]{3,2,0,1:T(8,128)(2,1)S(1)}, bf16[2,2,64,2048]{3,2,0,1:T(8,128)(2,1)S(1)}, u32[]{:S(2)}, u32[]{:S(2)}) collective-permute-start(bf16[2,2,64,2048]{3,2,0,1:T(8,128)(2,1)S(1)} %pad_maximum_fusion.5), channel_id=1, source_target_pairs={{0,2},{1,7},{2,4},{3,1},{4,6},{5,3},{6,0},{7,5},{8,10},{9,15},{10,... | collective-permute-start | bytes 3145736 | tf_op jit(solution)/shard_map/ppermute | solution.py:52
  128.3 9.3 %collective-permute-start.12 = (bf16[2,64,2048]{2,1,0:T(8,128)(2,1)S(1)}, bf16[2,64,2048]{2,1,0:T(8,128)(2,1)S(1)}, u32[]{:S(2)}, u32[]{:S(2)}) collective-permute-start(bf16[2,64,2048]{2,1,0:T(8,128)(2,1)S(1)} %slice_bitcast_fusion.2), channel_id=1, source_target_pairs={{0,2},{1,7},{2,4},{3,1},{4,6},{5,3},{6,0},{7,5},{8,10},{9,15},{10,... | collective-permute-start | bytes 1572872 | tf_op jit(solution)/shard_map/ppermute | solution.py:55
  131.5 9.0 %collective-permute-start.13 = (bf16[2,2,64,2048]{3,2,0,1:T(8,128)(2,1)S(1)}, bf16[2,2,64,2048]{3,2,0,1:T(8,128)(2,1)S(1)}, u32[]{:S(2)}, u32[]{:S(2)}) collective-permute-start(bf16[2,2,64,2048]{3,2,0,1:T(8,128)(2,1)S(1)} %collective-permute-done.11), channel_id=1, source_target_pairs={{0,1},{1,0},{2,3},{3,2},{4,5},{5,4},{6,7},{7,6},{8,9},{9,8},{10,11... | collective-permute-start | bytes 3145736 | tf_op jit(solution)/shard_map/ppermute | solution.py:56
  137.6 4.4 %collective-permute-start.14 = (bf16[2,64,2048]{2,1,0:T(8,128)(2,1)S(1)}, bf16[2,64,2048]{2,1,0:T(8,128)(2,1)S(1)}, u32[]{:S(2)}, u32[]{:S(2)}) collective-permute-start(bf16[2,64,2048]{2,1,0:T(8,128)(2,1)S(1)} %collective-permute-done.12), channel_id=1, source_target_pairs={{0,1},{1,0},{2,3},{3,2},{4,5},{5,4},{6,7},{7,6},{8,9},{9,8},{10,11... | collective-permute-start | bytes 1572872 | tf_op jit(solution)/shard_map/ppermute | solution.py:57
  142.0 1.9 %copy-start.4 = (f32[128,2]{0,1:T(2,128)S(1)}, f32[128,2]{0,1:T(2,128)}, u32[]{:S(2)}) copy-start(f32[128,2]{0,1:T(2,128)} %param.10) | copy-start | bytes 3076
